TPU v7x, 256 devices: a whole 4x4x8 slice. The times are simulated.
256 devices in a mesh: ctx: 256 (over z, y, x, core).
Axes of the slice: x: 4, y: 4, z: 8, core: 2. Of those that a mesh axis runs over, the one named last changes fastest.
Arguments:
- queries: bfloat16 [131072, 1024], P('ctx'), may hold values from -6 to 6
- key_rows: bfloat16 [131072, 128], P('ctx'), may hold values from -6 to 6
- value_rows: bfloat16 [131072, 128], P('ctx'), may hold values from -6 to 6
- grad_out: bfloat16 [131072, 1024], P('ctx'), may hold values from -16 to 16
- attn_out: bfloat16 [131072, 1024], P('ctx'), may hold values from -6 to 6
- log_total: float32 [8, 131072], P(None, 'ctx'), as said below
- block_pair: int32 [256], P('ctx'), may hold values from 0 to 255, as said below
Outputs:
- grad_queries: bfloat16 [131072, 1024], P('ctx')
- grad_keys: bfloat16 [131072, 128], P('ctx')
- grad_values: bfloat16 [131072, 128], P('ctx')
Inputs may be any that keep to these rules, and one draw needn't show every extreme that they name: `log_total`: the log of the sum of exp(scores) over the visible keys of each head and row. `block_pair`: each block number appears once.
All inputs are finite; a program needn't handle non-finite values.
Results may differ from a plain program's by a relative error of at most 0.0073.
Values may be sent and summed in bfloat16 or wider, within the bound.
No kernel may reach another device: no remote copies, remote signals or barrier semaphores. Data moves between devices by JAX's collectives and lax.ppermute only.
A program may use at most 64 MiB of HBM per device.

v0:
```python
import functools

import jax
import jax.numpy as jnp
from jax import lax
from jax.experimental import pallas as pl
from jax.experimental.pallas import tpu as pltpu
from jax.sharding import PartitionSpec as P


STEPS = 4


def passed_along(value, axis, steps):
    count = lax.axis_size(axis)
    pairs = [(source, (source + steps) % count) for source in range(count)]
    return lax.ppermute(value, axis, pairs)


def tile_body(tiles, has_in, own, group, half, width, scale,
              info_ref, q_ref, do_ref, kv_ref, lse_ref, dl_ref, *rest):
    if has_in:
        dqin_ref, *rest = rest
    if own:
        dq_ref, dk_ref, dv_ref, dlo_ref, acc_ref = rest
    else:
        dq_ref, dk_ref, dv_ref, acc_ref = rest
    block = pl.program_id(0)

    @pl.when(block == 0)
    def _():
        dk_ref[...] = jnp.zeros_like(dk_ref)
        dv_ref[...] = jnp.zeros_like(dv_ref)

    if has_in:
        acc_ref[...] = dqin_ref[...]
    else:
        acc_ref[...] = jnp.zeros_like(acc_ref)
    other = info_ref[0]
    lse_all = [lse_ref[pl.ds(block * group + j, 1), :] for j in range(group)]
    if own:
        dl_all = []
        for j in range(group):
            cols = pl.ds(j * width, width)
            prod = do_ref[:, cols].astype(jnp.float32) * dl_ref[:, cols].astype(jnp.float32)
            col = jnp.sum(prod, axis=1, keepdims=True)
            row = jnp.transpose(jnp.broadcast_to(col, (2 * half, width)))[0:1, :]
            dlo_ref[0, j:j + 1, :] = row
            dl_all.append(row)
    else:
        dl_all = [dl_ref[0, j:j + 1, :] for j in range(group)]
    for q_sel, k_sel, diag in tiles:
        if q_sel is None:
            qi = other
            lse = jnp.concatenate(
                [jnp.where(other == 0, x[:, :half], x[:, half:]) for x in lse_all], axis=1)
            dl = jnp.concatenate(
                [jnp.where(other == 0, x[:, :half], x[:, half:]) for x in dl_all], axis=1)
        else:
            qi = q_sel
            lanes = slice(q_sel * half, (q_sel + 1) * half)
            lse = jnp.concatenate([x[:, lanes] for x in lse_all], axis=1)
            dl = jnp.concatenate([x[:, lanes] for x in dl_all], axis=1)
        ki = other if k_sel is None else k_sel
        q_rows = pl.ds(pl.multiple_of(qi * half, half), half)
        k_rows = pl.ds(pl.multiple_of(ki * half, half), half)
        q = jnp.concatenate(
            [q_ref[q_rows, pl.ds(j * width, width)] for j in range(group)], axis=0)
        do = jnp.concatenate(
            [do_ref[q_rows, pl.ds(j * width, width)] for j in range(group)], axis=0)
        k = kv_ref[k_rows, pl.ds(0, width)]
        v = kv_ref[k_rows, pl.ds(width, width)]
        s_t = lax.dot_general(k, q, (((1,), (1,)), ((), ())),
                              preferred_element_type=jnp.float32) * scale
        p_t = jnp.exp(s_t - lse)
        if diag:
            rows = lax.broadcasted_iota(jnp.int32, (half, group * half), 0)
            cols_i = lax.broadcasted_iota(jnp.int32, (half, group * half), 1) % half
            p_t = jnp.where(rows <= cols_i, p_t, 0.0)
        dp_t = lax.dot_general(v, do, (((1,), (1,)), ((), ())),
                               preferred_element_type=jnp.float32)
        ds_t = (p_t * (dp_t - dl) * scale).astype(jnp.bfloat16)
        pb_t = p_t.astype(jnp.bfloat16)
        dv = jnp.dot(pb_t, do, preferred_element_type=jnp.float32)
        dk = jnp.dot(ds_t, q, preferred_element_type=jnp.float32)
        dq = lax.dot_general(ds_t, k, (((0,), (0,)), ((), ())),
                             preferred_element_type=jnp.float32)
        for j in range(group):
            acc_ref[q_rows, pl.ds(j * width, width)] += dq[j * half:(j + 1) * half]
        dk_ref[k_rows, :] += dk
        dv_ref[k_rows, :] += dv
    dq_ref[...] = acc_ref[...].astype(dq_ref.dtype)


GROUP = 4


def tile_step(tiles, info, queries, grad_out, kv, lse, delta, dq_in, dq_dtype):
    rows, cols = queries.shape
    width = kv.shape[1] // 2
    heads = cols // width
    half = rows // 2
    scale = width ** (-0.5)
    has_in = dq_in is not None
    own = delta.shape == queries.shape
    col_spec = pl.BlockSpec((rows, GROUP * width), lambda g, info: (0, g))
    kv_spec = pl.BlockSpec(kv.shape, lambda g, info: (0, 0))
    part_spec = pl.BlockSpec((rows, width), lambda g, info: (0, 0))
    row_spec = pl.BlockSpec((heads, rows), lambda g, info: (0, 0))
    group_spec = pl.BlockSpec((1, GROUP, rows), lambda g, info: (g, 0, 0))
    in_specs = [col_spec, col_spec, kv_spec, row_spec, col_spec if own else group_spec]
    args = [queries, grad_out, kv, lse, delta]
    aliases = {}
    if has_in:
        in_specs.append(col_spec)
        args.append(dq_in)
        if dq_in.dtype == dq_dtype:
            aliases = {len(args): 0}
    out_shape = [
        jax.ShapeDtypeStruct((rows, cols), dq_dtype),
        jax.ShapeDtypeStruct((rows, width), jnp.float32),
        jax.ShapeDtypeStruct((rows, width), jnp.float32),
    ]
    out_specs = [col_spec, part_spec, part_spec]
    if own:
        out_shape.append(jax.ShapeDtypeStruct((heads // GROUP, GROUP, rows), jnp.float32))
        out_specs.append(group_spec)
    flops = len(tiles) * heads * 5 * 2 * half * half * width
    nbytes = 2 * rows * cols * 2 + rows * 2 * width * 2 + rows * cols * 4 * (2 if has_in else 1)
    return pl.pallas_call(
        functools.partial(tile_body, tiles, has_in, own, GROUP, half, width, scale),
        out_shape=tuple(out_shape),
        grid_spec=pltpu.PrefetchScalarGridSpec(
            num_scalar_prefetch=1,
            grid=(heads // GROUP,),
            in_specs=in_specs,
            out_specs=out_specs,
            scratch_shapes=[pltpu.VMEM((rows, GROUP * width), jnp.float32)],
        ),
        input_output_aliases=aliases,
        compiler_params=pltpu.CompilerParams(dimension_semantics=("arbitrary",)),
        cost_estimate=pl.CostEstimate(
            flops=flops, transcendentals=len(tiles) * heads * half * half, bytes_accessed=nbytes
        ),
    )(info, *args)


OWN_TILES = ((0, 0, True), (1, 0, False), (1, 1, True))
VISIT_TILES = ((1, 0, False), (None, None, False))


def device_steps(queries, key_rows, value_rows, grad_out, attn_out, log_total, block_pair):
    rows, width = key_rows.shape
    own_block = block_pair[0]
    tag = jnp.broadcast_to(own_block.astype(jnp.bfloat16), (16, 2 * width))
    kv = jnp.concatenate([key_rows, value_rows], axis=1)
    kv = jnp.concatenate([kv, tag], axis=0)
    visitors = [kv]
    for _ in range(1, STEPS):
        visitors.append(passed_along(visitors[-1], "ctx", 1))

    zero_info = jnp.zeros((1,), jnp.int32)
    dq, sum_k, sum_v, delta = tile_step(OWN_TILES, zero_info, queries, grad_out, kv,
                                        log_total, attn_out, None, jnp.float32)
    for step in range(1, STEPS):
        got_k = passed_along(sum_k.astype(jnp.bfloat16), "ctx", 1).astype(jnp.float32)
        got_v = passed_along(sum_v.astype(jnp.bfloat16), "ctx", 1).astype(jnp.float32)
        kv_s = visitors[step]
        block_s = kv_s[rows, 0].astype(jnp.int32)
        other = jnp.where(block_s < own_block, 0, 1).astype(jnp.int32).reshape(1)
        last = step == STEPS - 1
        dq, part_k, part_v = tile_step(VISIT_TILES, other, queries, grad_out, kv_s,
                                       log_total, delta, dq,
                                       jnp.bfloat16 if last else jnp.float32)
        sum_k = got_k + part_k
        sum_v = got_v + part_v
    final_k = passed_along(sum_k.astype(jnp.bfloat16), "ctx", 1 - STEPS)
    final_v = passed_along(sum_v.astype(jnp.bfloat16), "ctx", 1 - STEPS)
    return dq, final_k, final_v


def solution(mesh):
    return jax.shard_map(
        device_steps,
        mesh=mesh,
        in_specs=(
            P("ctx", None),
            P("ctx", None),
            P("ctx", None),
            P("ctx", None),
            P("ctx", None),
            P(None, "ctx"),
            P("ctx"),
        ),
        out_specs=(P("ctx", None), P("ctx", None), P("ctx", None)),
        check_vma=False,
    )
```

profile of v0, /device:TPU:125, one launch (start us, length us, event | category | flops | bytes accessed | tf_op | source)
XLA Modules:
  0.0 63.4 jit_solution(4411357528684976401)
XLA Ops:
  1.3 1.0 %fusion.2.kv_ref = bf16[528,256]{1,0:T(8,128)(2,1)S(1)} fusion(bf16[512,128]{1,0:T(8,128)(2,1)} %param.9, bf16[512,128]{1,0:T(8,128)(2,1)} %param.8, bf16[]{:T(256)S(6)} %convert_element_type.63), kind=kLoop, calls=%fused_computation.3 | loop fusion | flops 946176 | bytes 532482 | tf_op jit(solution)/shard_map/concatenate | solution.py:156
  2.3 0.0 copy-start
  2.3 1.6 %collective-permute-start = (bf16[528,256]{1,0:T(8,128)(2,1)S(1)}, bf16[528,256]{1,0:T(8,128)(2,1)S(1)}, u32[]{:S(2)}, u32[]{:S(2)}) collective-permute-start(bf16[528,256]{1,0:T(8,128)(2,1)S(1)} %fusion.2.kv_ref), channel_id=1, source_target_pairs={{0,1},{1,2},{2,3},{3,4},{4,5},{5,6},{6,7},{7,8},{8,9},{9,10},{10,1... | collective-permute-start | bytes 811016 | tf_op jit(solution)/shard_map/ppermute | solution.py:17
  3.9 0.0 copy-done
  3.9 7.6 %shard_map.94 = (f32[512,1024]{1,0:T(8,128)}, f32[512,128]{1,0:T(8,128)}, f32[512,128]{1,0:T(8,128)}, f32[2,4,512]{2,1,0:T(4,128)}) custom-call(s32[1]{0:T(128)} %constant.2.clone.1.info_ref, bf16[512,1024]{1,0:T(8,128)(2,1)} %q_ref.7, bf16[512,1024]{1,0:T(8,128)(2,1)} %do_ref.7, bf16[528,256]{1,0:T(8,128)(2,1)} %copy-done, f32[8,512]{1,0:T(8,128)} %lse_ref.7, ...), custom_call_target="tpu_custom_call" | custom-call | flops 2013265920 | bytes 4456448 | tf_op jit(solution)/shard_map/pallas_call | solution.py:130
  11.4 1.0 %convert_element_type.70 = bf16[512,128]{1,0:T(8,128)(2,1)S(1)} convert(f32[512,128]{1,0:T(8,128)} %get-tuple-element.21) | non-fusion elementwise | flops 65536 | bytes 393216 | tf_op jit(solution)/shard_map/convert_element_type | solution.py:166
  12.4 0.7 %collective-permute-start.3 = (bf16[512,128]{1,0:T(8,128)(2,1)S(1)}, bf16[512,128]{1,0:T(8,128)(2,1)S(1)}, u32[]{:S(2)}, u32[]{:S(2)}) collective-permute-start(bf16[512,128]{1,0:T(8,128)(2,1)S(1)} %convert_element_type.70), channel_id=1, source_target_pairs={{0,1},{1,2},{2,3},{3,4},{4,5},{5,6},{6,7},{7,8},{8,9},{9,10},{10,1... | collective-permute-start | bytes 393224 | tf_op jit(solution)/shard_map/ppermute | solution.py:17
  13.1 1.0 %convert_element_type.77 = bf16[512,128]{1,0:T(8,128)(2,1)S(1)} convert(f32[512,128]{1,0:T(8,128)} %get-tuple-element.25) | non-fusion elementwise | flops 65536 | bytes 393216 | tf_op jit(solution)/shard_map/convert_element_type | solution.py:167
  14.0 2.3 %collective-permute-start.7 = (bf16[512,128]{1,0:T(8,128)(2,1)S(1)}, bf16[512,128]{1,0:T(8,128)(2,1)S(1)}, u32[]{:S(2)}, u32[]{:S(2)}) collective-permute-start(bf16[512,128]{1,0:T(8,128)(2,1)S(1)} %convert_element_type.77), channel_id=1, source_target_pairs={{0,1},{1,2},{2,3},{3,4},{4,5},{5,6},{6,7},{7,8},{8,9},{9,10},{10,1... | collective-permute-start | bytes 393224 | tf_op jit(solution)/shard_map/ppermute | solution.py:17
  16.3 0.0 collective-permute-done.kv_ref
  16.3 0.0 copy-start.2
  16.3 0.5 slice.14
  17.4 0.7 %collective-permute-start.1 = (bf16[528,256]{1,0:T(8,128)(2,1)S(1)}, bf16[528,256]{1,0:T(8,128)(2,1)S(1)}, u32[]{:S(2)}, u32[]{:S(2)}) collective-permute-start(bf16[528,256]{1,0:T(8,128)(2,1)S(1)} %collective-permute-done.kv_ref), channel_id=1, source_target_pairs={{0,1},{1,2},{2,3},{3,4},{4,5},{5,6},{6,7},{7,8},{8,9},{9,10},{10,1... | collective-permute-start | bytes 811016 | tf_op jit(solution)/shard_map/ppermute | solution.py:17
  18.1 0.0 copy-done.2
  18.1 6.3 %shard_map.95 = (f32[512,1024]{1,0:T(8,128)}, f32[512,128]{1,0:T(8,128)}, f32[512,128]{1,0:T(8,128)}) custom-call(s32[1]{0:T(128)} %bitcast.6.info_ref, bf16[512,1024]{1,0:T(8,128)(2,1)} %q_ref.7, bf16[512,1024]{1,0:T(8,128)(2,1)} %do_ref.7, bf16[528,256]{1,0:T(8,128)(2,1)} %copy-done.2, f32[8,512]{1,0:T(8,128)} %lse_ref.7, ...), custom_call_target="tpu_custom_call", output_to_operand_aliasing={{0}: (6, {})} | custom-call | flops 1342177280 | bytes 6553600 | tf_op jit(solution)/shard_map/pallas_call | solution.py:130
  24.4 0.0 collective-permute-done.3
  24.4 1.0 %add_convert_fusion.5 = bf16[512,128]{1,0:T(8,128)(2,1)S(1)} fusion(f32[512,128]{1,0:T(8,128)} %get-tuple-element.22, bf16[512,128]{1,0:T(8,128)(2,1)S(1)} %collective-permute-done.3), kind=kLoop, calls=%fused_computation.9 | loop fusion | flops 196608 | bytes 524288 | tf_op jit(solution)/shard_map/convert_element_type | solution.py:166
  25.4 1.1 %collective-permute-start.4 = (bf16[512,128]{1,0:T(8,128)(2,1)S(1)}, bf16[512,128]{1,0:T(8,128)(2,1)S(1)}, u32[]{:S(2)}, u32[]{:S(2)}) collective-permute-start(bf16[512,128]{1,0:T(8,128)(2,1)S(1)} %add_convert_fusion.5), channel_id=1, source_target_pairs={{0,1},{1,2},{2,3},{3,4},{4,5},{5,6},{6,7},{7,8},{8,9},{9,10},{10,1... | collective-permute-start | bytes 393224 | tf_op jit(solution)/shard_map/ppermute | solution.py:17
  26.4 0.0 collective-permute-done.7
  26.4 1.0 %add_convert_fusion.2 = bf16[512,128]{1,0:T(8,128)(2,1)S(1)} fusion(f32[512,128]{1,0:T(8,128)} %get-tuple-element.26, bf16[512,128]{1,0:T(8,128)(2,1)S(1)} %collective-permute-done.7), kind=kLoop, calls=%fused_computation.6 | loop fusion | flops 196608 | bytes 524288 | tf_op jit(solution)/shard_map/convert_element_type | solution.py:167
  27.4 0.7 %collective-permute-start.8 = (bf16[512,128]{1,0:T(8,128)(2,1)S(1)}, bf16[512,128]{1,0:T(8,128)(2,1)S(1)}, u32[]{:S(2)}, u32[]{:S(2)}) collective-permute-start(bf16[512,128]{1,0:T(8,128)(2,1)S(1)} %add_convert_fusion.2), channel_id=1, source_target_pairs={{0,1},{1,2},{2,3},{3,4},{4,5},{5,6},{6,7},{7,8},{8,9},{9,10},{10,1... | collective-permute-start | bytes 393224 | tf_op jit(solution)/shard_map/ppermute | solution.py:17
  28.1 0.0 collective-permute-done.1.kv_ref
  28.1 0.0 copy-start.1
  28.1 0.5 slice.13
  29.2 1.1 %collective-permute-start.2 = (bf16[528,256]{1,0:T(8,128)(2,1)S(1)}, bf16[528,256]{1,0:T(8,128)(2,1)S(1)}, u32[]{:S(2)}, u32[]{:S(2)}) collective-permute-start(bf16[528,256]{1,0:T(8,128)(2,1)S(1)} %collective-permute-done.1.kv_ref), channel_id=1, source_target_pairs={{0,1},{1,2},{2,3},{3,4},{4,5},{5,6},{6,7},{7,8},{8,9},{9,10},{10,1... | collective-permute-start | bytes 811016 | tf_op jit(solution)/shard_map/ppermute | solution.py:17
  30.3 0.0 copy-done.1
  30.3 6.3 %shard_map.96 = (f32[512,1024]{1,0:T(8,128)}, f32[512,128]{1,0:T(8,128)}, f32[512,128]{1,0:T(8,128)}) custom-call(s32[1]{0:T(128)} %bitcast.4.info_ref, bf16[512,1024]{1,0:T(8,128)(2,1)} %q_ref.7, bf16[512,1024]{1,0:T(8,128)(2,1)} %do_ref.7, bf16[528,256]{1,0:T(8,128)(2,1)} %copy-done.1, f32[8,512]{1,0:T(8,128)} %lse_ref.7, ...), custom_call_target="tpu_custom_call", output_to_operand_aliasing={{0}: (6, {})} | custom-call | flops 1342177280 | bytes 6553600 | tf_op jit(solution)/shard_map/pallas_call | solution.py:130
  36.6 0.0 collective-permute-done.4
  36.6 1.0 %add_convert_fusion.4 = bf16[512,128]{1,0:T(8,128)(2,1)S(1)} fusion(f32[512,128]{1,0:T(8,128)} %get-tuple-element.23, bf16[512,128]{1,0:T(8,128)(2,1)S(1)} %collective-permute-done.4), kind=kLoop, calls=%fused_computation.8 | loop fusion | flops 196608 | bytes 524288 | tf_op jit(solution)/shard_map/convert_element_type | solution.py:166
  37.5 0.9 %collective-permute-start.5 = (bf16[512,128]{1,0:T(8,128)(2,1)S(1)}, bf16[512,128]{1,0:T(8,128)(2,1)S(1)}, u32[]{:S(2)}, u32[]{:S(2)}) collective-permute-start(bf16[512,128]{1,0:T(8,128)(2,1)S(1)} %add_convert_fusion.4), channel_id=1, source_target_pairs={{0,1},{1,2},{2,3},{3,4},{4,5},{5,6},{6,7},{7,8},{8,9},{9,10},{10,1... | collective-permute-start | bytes 393224 | tf_op jit(solution)/shard_map/ppermute | solution.py:17
  38.4 0.0 collective-permute-done.8
  38.4 1.0 %add_convert_fusion.1 = bf16[512,128]{1,0:T(8,128)(2,1)S(1)} fusion(f32[512,128]{1,0:T(8,128)} %get-tuple-element.27, bf16[512,128]{1,0:T(8,128)(2,1)S(1)} %collective-permute-done.8), kind=kLoop, calls=%fused_computation.5 | loop fusion | flops 196608 | bytes 524288 | tf_op jit(solution)/shard_map/convert_element_type | solution.py:167
  39.4 1.4 %collective-permute-start.9 = (bf16[512,128]{1,0:T(8,128)(2,1)S(1)}, bf16[512,128]{1,0:T(8,128)(2,1)S(1)}, u32[]{:S(2)}, u32[]{:S(2)}) collective-permute-start(bf16[512,128]{1,0:T(8,128)(2,1)S(1)} %add_convert_fusion.1), channel_id=1, source_target_pairs={{0,1},{1,2},{2,3},{3,4},{4,5},{5,6},{6,7},{7,8},{8,9},{9,10},{10,1... | collective-permute-start | bytes 393224 | tf_op jit(solution)/shard_map/ppermute | solution.py:17
  40.8 0.0 collective-permute-done.2.kv_ref
  40.8 0.0 copy-start.3
  40.8 0.5 slice.12
  42.0 0.0 copy-done.3
  42.0 6.1 %shard_map.97 = (bf16[512,1024]{1,0:T(8,128)(2,1)}, f32[512,128]{1,0:T(8,128)}, f32[512,128]{1,0:T(8,128)}) custom-call(s32[1]{0:T(128)} %bitcast.2.info_ref, bf16[512,1024]{1,0:T(8,128)(2,1)} %q_ref.7, bf16[512,1024]{1,0:T(8,128)(2,1)} %do_ref.7, bf16[528,256]{1,0:T(8,128)(2,1)} %copy-done.3, f32[8,512]{1,0:T(8,128)} %lse_ref.7, ...), custom_call_target="tpu_custom_call" | custom-call | flops 1342177280 | bytes 6553600 | tf_op jit(solution)/shard_map/pallas_call | solution.py:130
  48.1 0.0 collective-permute-done.5
  48.1 1.0 %add_convert_fusion.3 = bf16[512,128]{1,0:T(8,128)(2,1)S(1)} fusion(f32[512,128]{1,0:T(8,128)} %get-tuple-element.24, bf16[512,128]{1,0:T(8,128)(2,1)S(1)} %collective-permute-done.5), kind=kLoop, calls=%fused_computation.7 | loop fusion | flops 196608 | bytes 524288 | tf_op jit(solution)/shard_map/convert_element_type | solution.py:177
  49.1 0.1 collective-permute-start.6
  49.1 0.0 collective-permute-done.9
  49.2 1.0 %add_convert_fusion = bf16[512,128]{1,0:T(8,128)(2,1)S(1)} fusion(f32[512,128]{1,0:T(8,128)} %get-tuple-element.28, bf16[512,128]{1,0:T(8,128)(2,1)S(1)} %collective-permute-done.9), kind=kLoop, calls=%fused_computation.4 | loop fusion | flops 196608 | bytes 524288 | tf_op jit(solution)/shard_map/convert_element_type | solution.py:178
  50.1 2.0 %collective-permute-start.10 = (bf16[512,128]{1,0:T(8,128)(2,1)S(1)}, bf16[512,128]{1,0:T(8,128)(2,1)S(1)}, u32[]{:S(2)}, u32[]{:S(2)}) collective-permute-start(bf16[512,128]{1,0:T(8,128)(2,1)S(1)} %add_convert_fusion), channel_id=1, source_target_pairs={{0,253},{1,254},{2,255},{3,0},{4,1},{5,2},{6,3},{7,4},{8,5},{9,6},... | collective-permute-start | bytes 393224 | tf_op jit(solution)/shard_map/ppermute | solution.py:17
  52.2 7.2 %collective-permute-done.6 = bf16[512,128]{1,0:T(8,128)(2,1)S(1)} collective-permute-done((bf16[512,128]{1,0:T(8,128)(2,1)S(1)}, bf16[512,128]{1,0:T(8,128)(2,1)S(1)}, u32[]{:S(2)}, u32[]{:S(2)}) %collective-permute-start.6) | collective-permute-done | bytes 131104 | tf_op jit(solution)/shard_map/ppermute | solution.py:17
  59.3 2.7 %collective-permute-done.10 = bf16[512,128]{1,0:T(8,128)(2,1)S(1)} collective-permute-done((bf16[512,128]{1,0:T(8,128)(2,1)S(1)}, bf16[512,128]{1,0:T(8,128)(2,1)S(1)}, u32[]{:S(2)}, u32[]{:S(2)}) %collective-permute-start.10) | collective-permute-done | bytes 131104 | tf_op jit(solution)/shard_map/ppermute | solution.py:17
  62.1 0.7 %copy.17 = bf16[512,128]{1,0:T(8,128)(2,1)} copy(bf16[512,128]{1,0:T(8,128)(2,1)S(1)} %collective-permute-done.6) | data formatting | bytes 262144
  62.7 0.7 %copy.18 = bf16[512,128]{1,0:T(8,128)(2,1)} copy(bf16[512,128]{1,0:T(8,128)(2,1)S(1)} %collective-permute-done.10) | data formatting | bytes 262144
Async XLA Ops:
  2.3 1.6 %copy-start = (bf16[528,256]{1,0:T(8,128)(2,1)}, bf16[528,256]{1,0:T(8,128)(2,1)S(1)}, u32[]{:S(2)}) copy-start(bf16[528,256]{1,0:T(8,128)(2,1)S(1)} %fusion.2.kv_ref) | copy-start | bytes 811012
  2.3 14.0 %collective-permute-start = (bf16[528,256]{1,0:T(8,128)(2,1)S(1)}, bf16[528,256]{1,0:T(8,128)(2,1)S(1)}, u32[]{:S(2)}, u32[]{:S(2)}) collective-permute-start(bf16[528,256]{1,0:T(8,128)(2,1)S(1)} %fusion.2.kv_ref), channel_id=1, source_target_pairs={{0,1},{1,2},{2,3},{3,4},{4,5},{5,6},{6,7},{7,8},{8,9},{9,10},{10,1... | collective-permute-start | bytes 811016 | tf_op jit(solution)/shard_map/ppermute | solution.py:17
  12.4 12.0 %collective-permute-start.3 = (bf16[512,128]{1,0:T(8,128)(2,1)S(1)}, bf16[512,128]{1,0:T(8,128)(2,1)S(1)}, u32[]{:S(2)}, u32[]{:S(2)}) collective-permute-start(bf16[512,128]{1,0:T(8,128)(2,1)S(1)} %convert_element_type.70), channel_id=1, source_target_pairs={{0,1},{1,2},{2,3},{3,4},{4,5},{5,6},{6,7},{7,8},{8,9},{9,10},{10,1... | collective-permute-start | bytes 393224 | tf_op jit(solution)/shard_map/ppermute | solution.py:17
  14.0 12.4 %collective-permute-start.7 = (bf16[512,128]{1,0:T(8,128)(2,1)S(1)}, bf16[512,128]{1,0:T(8,128)(2,1)S(1)}, u32[]{:S(2)}, u32[]{:S(2)}) collective-permute-start(bf16[512,128]{1,0:T(8,128)(2,1)S(1)} %convert_element_type.77), channel_id=1, source_target_pairs={{0,1},{1,2},{2,3},{3,4},{4,5},{5,6},{6,7},{7,8},{8,9},{9,10},{10,1... | collective-permute-start | bytes 393224 | tf_op jit(solution)/shard_map/ppermute | solution.py:17
  16.3 1.8 %copy-start.2 = (bf16[528,256]{1,0:T(8,128)(2,1)}, bf16[528,256]{1,0:T(8,128)(2,1)S(1)}, u32[]{:S(2)}) copy-start(bf16[528,256]{1,0:T(8,128)(2,1)S(1)} %collective-permute-done.kv_ref) | copy-start | bytes 811012
  17.4 10.7 %collective-permute-start.1 = (bf16[528,256]{1,0:T(8,128)(2,1)S(1)}, bf16[528,256]{1,0:T(8,128)(2,1)S(1)}, u32[]{:S(2)}, u32[]{:S(2)}) collective-permute-start(bf16[528,256]{1,0:T(8,128)(2,1)S(1)} %collective-permute-done.kv_ref), channel_id=1, source_target_pairs={{0,1},{1,2},{2,3},{3,4},{4,5},{5,6},{6,7},{7,8},{8,9},{9,10},{10,1... | collective-permute-start | bytes 811016 | tf_op jit(solution)/shard_map/ppermute | solution.py:17
  25.4 11.2 %collective-permute-start.4 = (bf16[512,128]{1,0:T(8,128)(2,1)S(1)}, bf16[512,128]{1,0:T(8,128)(2,1)S(1)}, u32[]{:S(2)}, u32[]{:S(2)}) collective-permute-start(bf16[512,128]{1,0:T(8,128)(2,1)S(1)} %add_convert_fusion.5), channel_id=1, source_target_pairs={{0,1},{1,2},{2,3},{3,4},{4,5},{5,6},{6,7},{7,8},{8,9},{9,10},{10,1... | collective-permute-start | bytes 393224 | tf_op jit(solution)/shard_map/ppermute | solution.py:17
  27.4 11.0 %collective-permute-start.8 = (bf16[512,128]{1,0:T(8,128)(2,1)S(1)}, bf16[512,128]{1,0:T(8,128)(2,1)S(1)}, u32[]{:S(2)}, u32[]{:S(2)}) collective-permute-start(bf16[512,128]{1,0:T(8,128)(2,1)S(1)} %add_convert_fusion.2), channel_id=1, source_target_pairs={{0,1},{1,2},{2,3},{3,4},{4,5},{5,6},{6,7},{7,8},{8,9},{9,10},{10,1... | collective-permute-start | bytes 393224 | tf_op jit(solution)/shard_map/ppermute | solution.py:17
  28.1 2.2 %copy-start.1 = (bf16[528,256]{1,0:T(8,128)(2,1)}, bf16[528,256]{1,0:T(8,128)(2,1)S(1)}, u32[]{:S(2)}) copy-start(bf16[528,256]{1,0:T(8,128)(2,1)S(1)} %collective-permute-done.1.kv_ref) | copy-start | bytes 811012
  29.2 11.6 %collective-permute-start.2 = (bf16[528,256]{1,0:T(8,128)(2,1)S(1)}, bf16[528,256]{1,0:T(8,128)(2,1)S(1)}, u32[]{:S(2)}, u32[]{:S(2)}) collective-permute-start(bf16[528,256]{1,0:T(8,128)(2,1)S(1)} %collective-permute-done.1.kv_ref), channel_id=1, source_target_pairs={{0,1},{1,2},{2,3},{3,4},{4,5},{5,6},{6,7},{7,8},{8,9},{9,10},{10,1... | collective-permute-start | bytes 811016 | tf_op jit(solution)/shard_map/ppermute | solution.py:17
  37.5 10.5 %collective-permute-start.5 = (bf16[512,128]{1,0:T(8,128)(2,1)S(1)}, bf16[512,128]{1,0:T(8,128)(2,1)S(1)}, u32[]{:S(2)}, u32[]{:S(2)}) collective-permute-start(bf16[512,128]{1,0:T(8,128)(2,1)S(1)} %add_convert_fusion.4), channel_id=1, source_target_pairs={{0,1},{1,2},{2,3},{3,4},{4,5},{5,6},{6,7},{7,8},{8,9},{9,10},{10,1... | collective-permute-start | bytes 393224 | tf_op jit(solution)/shard_map/ppermute | solution.py:17
  39.4 9.7 %collective-permute-start.9 = (bf16[512,128]{1,0:T(8,128)(2,1)S(1)}, bf16[512,128]{1,0:T(8,128)(2,1)S(1)}, u32[]{:S(2)}, u32[]{:S(2)}) collective-permute-start(bf16[512,128]{1,0:T(8,128)(2,1)S(1)} %add_convert_fusion.1), channel_id=1, source_target_pairs={{0,1},{1,2},{2,3},{3,4},{4,5},{5,6},{6,7},{7,8},{8,9},{9,10},{10,1... | collective-permute-start | bytes 393224 | tf_op jit(solution)/shard_map/ppermute | solution.py:17
  40.8 1.2 %copy-start.3 = (bf16[528,256]{1,0:T(8,128)(2,1)}, bf16[528,256]{1,0:T(8,128)(2,1)S(1)}, u32[]{:S(2)}) copy-start(bf16[528,256]{1,0:T(8,128)(2,1)S(1)} %collective-permute-done.2.kv_ref) | copy-start | bytes 811012
  49.1 10.3 %collective-permute-start.6 = (bf16[512,128]{1,0:T(8,128)(2,1)S(1)}, bf16[512,128]{1,0:T(8,128)(2,1)S(1)}, u32[]{:S(2)}, u32[]{:S(2)}) collective-permute-start(bf16[512,128]{1,0:T(8,128)(2,1)S(1)} %add_convert_fusion.3), channel_id=1, source_target_pairs={{0,253},{1,254},{2,255},{3,0},{4,1},{5,2},{6,3},{7,4},{8,5},{9,6},... | collective-permute-start | bytes 393224 | tf_op jit(solution)/shard_map/ppermute | solution.py:17
  50.1 11.9 %collective-permute-start.10 = (bf16[512,128]{1,0:T(8,128)(2,1)S(1)}, bf16[512,128]{1,0:T(8,128)(2,1)S(1)}, u32[]{:S(2)}, u32[]{:S(2)}) collective-permute-start(bf16[512,128]{1,0:T(8,128)(2,1)S(1)} %add_convert_fusion), channel_id=1, source_target_pairs={{0,253},{1,254},{2,255},{3,0},{4,1},{5,2},{6,3},{7,4},{8,5},{9,6},... | collective-permute-start | bytes 393224 | tf_op jit(solution)/shard_map/ppermute | solution.py:17
where the time goes:
time: 64.4 us; the launch traced here: 63.4 us
  Pallas kernels  26.1 us (41%)
  starting transfers between devices  12.4 us (19%)
  waiting for transfers between devices  9.93 us (15%)
  other arithmetic  8.83 us (14%)
  between operations  3.19 us (5%)
  local copies, waits for them, and re-layouts  2.91 us (5%)
    pallas_call x4, Pallas kernels, tile_step(): pl.pallas_call(functools.partial(tile_body, tiles, has_in, own, GROUP, ha...  26.1 us
    ppermute x11, starting transfers between devices, passed_along(): return lax.ppermute(value, axis, pairs)  12.4 us
    ppermute x11, waiting for transfers between devices, passed_along(): return lax.ppermute(value, axis, pairs)  9.93 us
    convert_element_type x3, other arithmetic, device_steps(): sum_k.astype(jnp.bfloat16)  2.94 us
    convert_element_type x3, other arithmetic, device_steps(): sum_v.astype(jnp.bfloat16)  2.93 us
    slice x3, local copies, waits for them, and re-layouts, device_steps(): block_s = kv_s[rows, 0].astype(jnp.int32)  1.58 us
    unnamed x10, local copies, waits for them, and re-layouts  1.33 us
  transfers between devices with their start and end apart: 11, of which 2 were waited for; matrix products, arithmetic and copies ran while one was open for 15% of the time, Pallas kernels for 41%

commit v1 on v0

--- a/solution.py
+++ b/solution.py
@@ -36,7 +36,6 @@
         acc_ref[...] = dqin_ref[...]
     else:
         acc_ref[...] = jnp.zeros_like(acc_ref)
-    other = info_ref[0]
     lse_all = [lse_ref[pl.ds(block * group + j, 1), :] for j in range(group)]
     if own:
         dl_all = []
@@ -49,27 +48,29 @@
             dl_all.append(row)
     else:
         dl_all = [dl_ref[0, j:j + 1, :] for j in range(group)]
+    if own:
+        upper = None
+    else:
+        seen = kv_ref[pl.ds(2 * half, 1), pl.ds(0, 2 * width)].astype(jnp.float32)
+        mine = jnp.full((1, 2 * width), info_ref[0], jnp.int32).astype(jnp.float32)
+        upper = (seen > mine)[:, 0:1]
+    lo_rows, hi_rows = pl.ds(0, half), pl.ds(half, half)
     for q_sel, k_sel, diag in tiles:
-        if q_sel is None:
-            qi = other
-            lse = jnp.concatenate(
-                [jnp.where(other == 0, x[:, :half], x[:, half:]) for x in lse_all], axis=1)
-            dl = jnp.concatenate(
-                [jnp.where(other == 0, x[:, :half], x[:, half:]) for x in dl_all], axis=1)
-        else:
-            qi = q_sel
-            lanes = slice(q_sel * half, (q_sel + 1) * half)
-            lse = jnp.concatenate([x[:, lanes] for x in lse_all], axis=1)
-            dl = jnp.concatenate([x[:, lanes] for x in dl_all], axis=1)
-        ki = other if k_sel is None else k_sel
-        q_rows = pl.ds(pl.multiple_of(qi * half, half), half)
-        k_rows = pl.ds(pl.multiple_of(ki * half, half), half)
+        def pick(hi, lo, sel=q_sel):
+            if sel is None:
+                return jnp.where(upper, hi, lo)
+            return hi if sel == 1 else lo
+
+        lse = jnp.concatenate([pick(x[:, half:], x[:, :half]) for x in lse_all], axis=1)
+        dl = jnp.concatenate([pick(x[:, half:], x[:, :half]) for x in dl_all], axis=1)
         q = jnp.concatenate(
-            [q_ref[q_rows, pl.ds(j * width, width)] for j in range(group)], axis=0)
+            [pick(q_ref[hi_rows, pl.ds(j * width, width)], q_ref[lo_rows, pl.ds(j * width, width)])
+             for j in range(group)], axis=0)
         do = jnp.concatenate(
-            [do_ref[q_rows, pl.ds(j * width, width)] for j in range(group)], axis=0)
-        k = kv_ref[k_rows, pl.ds(0, width)]
-        v = kv_ref[k_rows, pl.ds(width, width)]
+            [pick(do_ref[hi_rows, pl.ds(j * width, width)], do_ref[lo_rows, pl.ds(j * width, width)])
+             for j in range(group)], axis=0)
+        k = pick(kv_ref[hi_rows, pl.ds(0, width)], kv_ref[lo_rows, pl.ds(0, width)], k_sel)
+        v = pick(kv_ref[hi_rows, pl.ds(width, width)], kv_ref[lo_rows, pl.ds(width, width)], k_sel)
         s_t = lax.dot_general(k, q, (((1,), (1,)), ((), ())),
                               preferred_element_type=jnp.float32) * scale
         p_t = jnp.exp(s_t - lse)
@@ -85,10 +86,18 @@
         dk = jnp.dot(ds_t, q, preferred_element_type=jnp.float32)
         dq = lax.dot_general(ds_t, k, (((0,), (0,)), ((), ())),
                              preferred_element_type=jnp.float32)
+
+        def add_to(ref, cols, value, sel):
+            if sel is None:
+                ref[hi_rows, cols] += jnp.where(upper, value, 0.0)
+                ref[lo_rows, cols] += jnp.where(upper, 0.0, value)
+            else:
+                ref[hi_rows if sel == 1 else lo_rows, cols] += value
+
         for j in range(group):
-            acc_ref[q_rows, pl.ds(j * width, width)] += dq[j * half:(j + 1) * half]
-        dk_ref[k_rows, :] += dk
-        dv_ref[k_rows, :] += dv
+            add_to(acc_ref, pl.ds(j * width, width), dq[j * half:(j + 1) * half], q_sel)
+        add_to(dk_ref, pl.ds(0, width), dk, k_sel)
+        add_to(dv_ref, pl.ds(0, width), dv, k_sel)
     dq_ref[...] = acc_ref[...].astype(dq_ref.dtype)
 
 
@@ -150,7 +159,7 @@
 
 
 def device_steps(queries, key_rows, value_rows, grad_out, attn_out, log_total, block_pair):
-    rows, width = key_rows.shape
+    _, width = key_rows.shape
     own_block = block_pair[0]
     tag = jnp.broadcast_to(own_block.astype(jnp.bfloat16), (16, 2 * width))
     kv = jnp.concatenate([key_rows, value_rows], axis=1)
@@ -159,17 +168,15 @@
     for _ in range(1, STEPS):
         visitors.append(passed_along(visitors[-1], "ctx", 1))
 
-    zero_info = jnp.zeros((1,), jnp.int32)
-    dq, sum_k, sum_v, delta = tile_step(OWN_TILES, zero_info, queries, grad_out, kv,
+    own_info = block_pair
+    dq, sum_k, sum_v, delta = tile_step(OWN_TILES, own_info, queries, grad_out, kv,
                                         log_total, attn_out, None, jnp.float32)
     for step in range(1, STEPS):
-        got_k = passed_along(sum_k.astype(jnp.bfloat16), "ctx", 1).astype(jnp.float32)
-        got_v = passed_along(sum_v.astype(jnp.bfloat16), "ctx", 1).astype(jnp.float32)
+        got_k = passed_along(sum_k, "ctx", 1)
+        got_v = passed_along(sum_v, "ctx", 1)
         kv_s = visitors[step]
-        block_s = kv_s[rows, 0].astype(jnp.int32)
-        other = jnp.where(block_s < own_block, 0, 1).astype(jnp.int32).reshape(1)
         last = step == STEPS - 1
-        dq, part_k, part_v = tile_step(VISIT_TILES, other, queries, grad_out, kv_s,
+        dq, part_k, part_v = tile_step(VISIT_TILES, own_info, queries, grad_out, kv_s,
                                        log_total, delta, dq,
                                        jnp.bfloat16 if last else jnp.float32)
         sum_k = got_k + part_k

time: 64.4 us -> 65.3 us (1.014)
  the two profiles are of different devices: /device:TPU:125 before, /device:TPU:2 now
where the time goes in v1:
time: 65.3 us; the launch traced here: 65 us
  Pallas kernels  25.9 us (40%)
  starting transfers between devices  23.4 us (36%)
  other arithmetic  6.88 us (11%)
  waiting for transfers between devices  4.93 us (8%)
  local copies, waits for them, and re-layouts  2.64 us (4%)
  between operations  1.35 us (2%)
    pallas_call x4, Pallas kernels, tile_step(): pl.pallas_call(functools.partial(tile_body, tiles, has_in, own, GROUP, ha...  25.9 us
    ppermute x11, starting transfers between devices, passed_along(): return lax.ppermute(value, axis, pairs)  23.4 us
    ppermute x11, waiting for transfers between devices, passed_along(): return lax.ppermute(value, axis, pairs)  4.93 us
    unnamed x10, local copies, waits for them, and re-layouts  2.64 us
    add x2, other arithmetic, device_steps(): sum_v = got_v + part_v  1.96 us
    add x2, other arithmetic, device_steps(): sum_k = got_k + part_k  1.96 us
  transfers between devices with their start and end apart: 11, of which 3 were waited for; matrix products, arithmetic and copies ran while one was open for 9% of the time, Pallas kernels for 40%

profile of v1, /device:TPU:2, one launch (start us, length us, event | category | flops | bytes accessed | tf_op | source)
XLA Modules:
  0.0 65.0 jit_solution(1365118957043252830)
XLA Ops:
  1.3 1.0 %fusion.2.kv_ref = bf16[528,256]{1,0:T(8,128)(2,1)S(1)} fusion(bf16[512,128]{1,0:T(8,128)(2,1)} %param.9, bf16[512,128]{1,0:T(8,128)(2,1)} %param.8, bf16[]{:T(256)} %bitcast), kind=kLoop, calls=%fused_computation.3 | loop fusion | flops 946176 | bytes 532482 | tf_op jit(solution)/shard_map/concatenate | solution.py:165
  2.3 0.0 copy-start
  2.3 0.1 collective-permute-start
  2.4 0.6 copy-done
  3.0 7.5 %shard_map.94 = (f32[512,1024]{1,0:T(8,128)}, f32[512,128]{1,0:T(8,128)}, f32[512,128]{1,0:T(8,128)}, f32[2,4,512]{2,1,0:T(4,128)}) custom-call(s32[1]{0:T(128)S(6)} %copy.16.info_ref, bf16[512,1024]{1,0:T(8,128)(2,1)} %q_ref.7, bf16[512,1024]{1,0:T(8,128)(2,1)} %do_ref.7, bf16[528,256]{1,0:T(8,128)(2,1)} %copy-done, f32[8,512]{1,0:T(8,128)} %lse_ref.7, ...), custom_call_target="tpu_custom_call" | custom-call | flops 2013265920 | bytes 4456448 | tf_op jit(solution)/shard_map/pallas_call | solution.py:139
  10.5 1.0 %collective-permute-start.7 = (f32[512,128]{1,0:T(8,128)}, f32[512,128]{1,0:T(8,128)S(1)}, u32[]{:S(2)}, u32[]{:S(2)}) collective-permute-start(f32[512,128]{1,0:T(8,128)} %get-tuple-element.25), channel_id=1, source_target_pairs={{0,1},{1,2},{2,3},{3,4},{4,5},{5,6},{6,7},{7,8},{8,9},{9,10},{10,1... | collective-permute-start | bytes 786440 | tf_op jit(solution)/shard_map/ppermute | solution.py:17
  11.5 0.0 collective-permute-done.kv_ref
  11.5 0.0 copy-start.3
  11.5 0.6 collective-permute-start.1
  12.2 0.7 %collective-permute-start.3 = (f32[512,128]{1,0:T(8,128)}, f32[512,128]{1,0:T(8,128)S(1)}, u32[]{:S(2)}, u32[]{:S(2)}) collective-permute-start(f32[512,128]{1,0:T(8,128)} %get-tuple-element.21), channel_id=1, source_target_pairs={{0,1},{1,2},{2,3},{3,4},{4,5},{5,6},{6,7},{7,8},{8,9},{9,10},{10,1... | collective-permute-start | bytes 786440 | tf_op jit(solution)/shard_map/ppermute | solution.py:17
  12.9 0.0 copy-done.3
  12.9 6.2 %shard_map.95 = (f32[512,1024]{1,0:T(8,128)}, f32[512,128]{1,0:T(8,128)}, f32[512,128]{1,0:T(8,128)}) custom-call(s32[1]{0:T(128)S(6)} %copy.16.info_ref, bf16[512,1024]{1,0:T(8,128)(2,1)} %q_ref.7, bf16[512,1024]{1,0:T(8,128)(2,1)} %do_ref.7, bf16[528,256]{1,0:T(8,128)(2,1)} %copy-done.3, f32[8,512]{1,0:T(8,128)} %lse_ref.7, ...), custom_call_target="tpu_custom_call", output_to_operand_aliasing={{0}: (6, {})} | custom-call | flops 1342177280 | bytes 6553600 | tf_op jit(solution)/shard_map/pallas_call | solution.py:139
  19.0 0.0 collective-permute-done.7
  19.0 1.0 %add.23 = f32[512,128]{1,0:T(8,128)S(1)} add(f32[512,128]{1,0:T(8,128)S(1)} %collective-permute-done.7, f32[512,128]{1,0:T(8,128)} %get-tuple-element.26) | non-fusion elementwise | flops 65536 | bytes 786432 | tf_op jit(solution)/shard_map/add | solution.py:183
  20.0 0.7 %collective-permute-start.8 = (f32[512,128]{1,0:T(8,128)S(1)}, f32[512,128]{1,0:T(8,128)S(1)}, u32[]{:S(2)}, u32[]{:S(2)}) collective-permute-start(f32[512,128]{1,0:T(8,128)S(1)} %add.23), channel_id=1, source_target_pairs={{0,1},{1,2},{2,3},{3,4},{4,5},{5,6},{6,7},{7,8},{8,9},{9,10},{10,1... | collective-permute-start | bytes 786440 | tf_op jit(solution)/shard_map/ppermute | solution.py:17
  20.7 0.0 collective-permute-done.1.kv_ref
  20.7 0.0 copy-start.1
  20.7 1.0 %collective-permute-start.2 = (bf16[528,256]{1,0:T(8,128)(2,1)S(1)}, bf16[528,256]{1,0:T(8,128)(2,1)S(1)}, u32[]{:S(2)}, u32[]{:S(2)}) collective-permute-start(bf16[528,256]{1,0:T(8,128)(2,1)S(1)} %collective-permute-done.1.kv_ref), channel_id=1, source_target_pairs={{0,1},{1,2},{2,3},{3,4},{4,5},{5,6},{6,7},{7,8},{8,9},{9,10},{10,1... | collective-permute-start | bytes 811016 | tf_op jit(solution)/shard_map/ppermute | solution.py:17
  21.7 0.5 collective-permute-done.3
  22.3 1.0 %add.20 = f32[512,128]{1,0:T(8,128)S(1)} add(f32[512,128]{1,0:T(8,128)S(1)} %collective-permute-done.3, f32[512,128]{1,0:T(8,128)} %get-tuple-element.22) | non-fusion elementwise | flops 65536 | bytes 786432 | tf_op jit(solution)/shard_map/add | solution.py:182
  23.2 0.1 collective-permute-start.4
  23.4 0.0 copy-done.1
  23.4 6.2 %shard_map.96 = (f32[512,1024]{1,0:T(8,128)}, f32[512,128]{1,0:T(8,128)}, f32[512,128]{1,0:T(8,128)}) custom-call(s32[1]{0:T(128)S(6)} %copy.16.info_ref, bf16[512,1024]{1,0:T(8,128)(2,1)} %q_ref.7, bf16[512,1024]{1,0:T(8,128)(2,1)} %do_ref.7, bf16[528,256]{1,0:T(8,128)(2,1)} %copy-done.1, f32[8,512]{1,0:T(8,128)} %lse_ref.7, ...), custom_call_target="tpu_custom_call", output_to_operand_aliasing={{0}: (6, {})} | custom-call | flops 1342177280 | bytes 6553600 | tf_op jit(solution)/shard_map/pallas_call | solution.py:139
  29.5 0.0 collective-permute-done.8
  29.6 1.0 %add.24 = f32[512,128]{1,0:T(8,128)S(1)} add(f32[512,128]{1,0:T(8,128)S(1)} %collective-permute-done.8, f32[512,128]{1,0:T(8,128)} %get-tuple-element.27) | non-fusion elementwise | flops 65536 | bytes 786432 | tf_op jit(solution)/shard_map/add | solution.py:183
  30.5 1.8 %collective-permute-start.9 = (f32[512,128]{1,0:T(8,128)S(1)}, f32[512,128]{1,0:T(8,128)S(1)}, u32[]{:S(2)}, u32[]{:S(2)}) collective-permute-start(f32[512,128]{1,0:T(8,128)S(1)} %add.24), channel_id=1, source_target_pairs={{0,1},{1,2},{2,3},{3,4},{4,5},{5,6},{6,7},{7,8},{8,9},{9,10},{10,1... | collective-permute-start | bytes 786440 | tf_op jit(solution)/shard_map/ppermute | solution.py:17
  32.3 0.0 collective-permute-done.4
  32.3 1.0 %add.21 = f32[512,128]{1,0:T(8,128)S(1)} add(f32[512,128]{1,0:T(8,128)S(1)} %collective-permute-done.4, f32[512,128]{1,0:T(8,128)} %get-tuple-element.23) | non-fusion elementwise | flops 65536 | bytes 786432 | tf_op jit(solution)/shard_map/add | solution.py:182
  33.3 0.2 collective-permute-start.5
  33.5 0.0 collective-permute-done.2.kv_ref
  33.5 0.0 copy-start.2
  33.5 0.7 %copy-done.2 = bf16[528,256]{1,0:T(8,128)(2,1)} copy-done((bf16[528,256]{1,0:T(8,128)(2,1)}, bf16[528,256]{1,0:T(8,128)(2,1)S(1)}, u32[]{:S(2)}) %copy-start.2) | copy-done | bytes 270360
  34.2 6.0 %shard_map.97 = (bf16[512,1024]{1,0:T(8,128)(2,1)}, f32[512,128]{1,0:T(8,128)}, f32[512,128]{1,0:T(8,128)}) custom-call(s32[1]{0:T(128)S(6)} %copy.16.info_ref, bf16[512,1024]{1,0:T(8,128)(2,1)} %q_ref.7, bf16[512,1024]{1,0:T(8,128)(2,1)} %do_ref.7, bf16[528,256]{1,0:T(8,128)(2,1)} %copy-done.2, f32[8,512]{1,0:T(8,128)} %lse_ref.7, ...), custom_call_target="tpu_custom_call" | custom-call | flops 1342177280 | bytes 6553600 | tf_op jit(solution)/shard_map/pallas_call | solution.py:139
  40.2 0.0 collective-permute-done.9
  40.2 1.0 %add_convert_fusion = bf16[512,128]{1,0:T(8,128)(2,1)S(1)} fusion(f32[512,128]{1,0:T(8,128)S(1)} %collective-permute-done.9, f32[512,128]{1,0:T(8,128)} %get-tuple-element.28), kind=kLoop, calls=%fused_computation.4 | loop fusion | flops 131072 | bytes 655360 | tf_op jit(solution)/shard_map/convert_element_type | solution.py:185
  41.1 17.1 %collective-permute-start.10 = (bf16[512,128]{1,0:T(8,128)(2,1)S(1)}, bf16[512,128]{1,0:T(8,128)(2,1)S(1)}, u32[]{:S(2)}, u32[]{:S(2)}) collective-permute-start(bf16[512,128]{1,0:T(8,128)(2,1)S(1)} %add_convert_fusion), channel_id=1, source_target_pairs={{0,253},{1,254},{2,255},{3,0},{4,1},{5,2},{6,3},{7,4},{8,5},{9,6},... | collective-permute-start | bytes 393224 | tf_op jit(solution)/shard_map/ppermute | solution.py:17
  58.2 0.0 collective-permute-done.5
  58.2 1.0 %add_convert_fusion.1 = bf16[512,128]{1,0:T(8,128)(2,1)S(1)} fusion(f32[512,128]{1,0:T(8,128)S(1)} %collective-permute-done.5, f32[512,128]{1,0:T(8,128)} %get-tuple-element.24), kind=kLoop, calls=%fused_computation.5 | loop fusion | flops 131072 | bytes 655360 | tf_op jit(solution)/shard_map/convert_element_type | solution.py:184
  59.2 0.1 collective-permute-start.6
  59.3 1.4 %collective-permute-done.10 = bf16[512,128]{1,0:T(8,128)(2,1)S(1)} collective-permute-done((bf16[512,128]{1,0:T(8,128)(2,1)S(1)}, bf16[512,128]{1,0:T(8,128)(2,1)S(1)}, u32[]{:S(2)}, u32[]{:S(2)}) %collective-permute-start.10) | collective-permute-done | bytes 131104 | tf_op jit(solution)/shard_map/ppermute | solution.py:17
  60.8 2.9 %collective-permute-done.6 = bf16[512,128]{1,0:T(8,128)(2,1)S(1)} collective-permute-done((bf16[512,128]{1,0:T(8,128)(2,1)S(1)}, bf16[512,128]{1,0:T(8,128)(2,1)S(1)}, u32[]{:S(2)}, u32[]{:S(2)}) %collective-permute-start.6) | collective-permute-done | bytes 131104 | tf_op jit(solution)/shard_map/ppermute | solution.py:17
  63.7 0.7 %copy.17 = bf16[512,128]{1,0:T(8,128)(2,1)} copy(bf16[512,128]{1,0:T(8,128)(2,1)S(1)} %collective-permute-done.6) | data formatting | bytes 262144
  64.3 0.7 %copy.18 = bf16[512,128]{1,0:T(8,128)(2,1)} copy(bf16[512,128]{1,0:T(8,128)(2,1)S(1)} %collective-permute-done.10) | data formatting | bytes 262144
Async XLA Ops:
  2.3 0.7 %copy-start = (bf16[528,256]{1,0:T(8,128)(2,1)}, bf16[528,256]{1,0:T(8,128)(2,1)S(1)}, u32[]{:S(2)}) copy-start(bf16[528,256]{1,0:T(8,128)(2,1)S(1)} %fusion.2.kv_ref) | copy-start | bytes 811012
  2.3 9.2 %collective-permute-start = (bf16[528,256]{1,0:T(8,128)(2,1)S(1)}, bf16[528,256]{1,0:T(8,128)(2,1)S(1)}, u32[]{:S(2)}, u32[]{:S(2)}) collective-permute-start(bf16[528,256]{1,0:T(8,128)(2,1)S(1)} %fusion.2.kv_ref), channel_id=1, source_target_pairs={{0,1},{1,2},{2,3},{3,4},{4,5},{5,6},{6,7},{7,8},{8,9},{9,10},{10,1... | collective-permute-start | bytes 811016 | tf_op jit(solution)/shard_map/ppermute | solution.py:17
  10.5 8.5 %collective-permute-start.7 = (f32[512,128]{1,0:T(8,128)}, f32[512,128]{1,0:T(8,128)S(1)}, u32[]{:S(2)}, u32[]{:S(2)}) collective-permute-start(f32[512,128]{1,0:T(8,128)} %get-tuple-element.25), channel_id=1, source_target_pairs={{0,1},{1,2},{2,3},{3,4},{4,5},{5,6},{6,7},{7,8},{8,9},{9,10},{10,1... | collective-permute-start | bytes 786440 | tf_op jit(solution)/shard_map/ppermute | solution.py:17
  11.5 1.3 %copy-start.3 = (bf16[528,256]{1,0:T(8,128)(2,1)}, bf16[528,256]{1,0:T(8,128)(2,1)S(1)}, u32[]{:S(2)}) copy-start(bf16[528,256]{1,0:T(8,128)(2,1)S(1)} %collective-permute-done.kv_ref) | copy-start | bytes 811012
  11.5 9.2 %collective-permute-start.1 = (bf16[528,256]{1,0:T(8,128)(2,1)S(1)}, bf16[528,256]{1,0:T(8,128)(2,1)S(1)}, u32[]{:S(2)}, u32[]{:S(2)}) collective-permute-start(bf16[528,256]{1,0:T(8,128)(2,1)S(1)} %collective-permute-done.kv_ref), channel_id=1, source_target_pairs={{0,1},{1,2},{2,3},{3,4},{4,5},{5,6},{6,7},{7,8},{8,9},{9,10},{10,1... | collective-permute-start | bytes 811016 | tf_op jit(solution)/shard_map/ppermute | solution.py:17
  12.2 10.1 %collective-permute-start.3 = (f32[512,128]{1,0:T(8,128)}, f32[512,128]{1,0:T(8,128)S(1)}, u32[]{:S(2)}, u32[]{:S(2)}) collective-permute-start(f32[512,128]{1,0:T(8,128)} %get-tuple-element.21), channel_id=1, source_target_pairs={{0,1},{1,2},{2,3},{3,4},{4,5},{5,6},{6,7},{7,8},{8,9},{9,10},{10,1... | collective-permute-start | bytes 786440 | tf_op jit(solution)/shard_map/ppermute | solution.py:17
  20.0 9.5 %collective-permute-start.8 = (f32[512,128]{1,0:T(8,128)S(1)}, f32[512,128]{1,0:T(8,128)S(1)}, u32[]{:S(2)}, u32[]{:S(2)}) collective-permute-start(f32[512,128]{1,0:T(8,128)S(1)} %add.23), channel_id=1, source_target_pairs={{0,1},{1,2},{2,3},{3,4},{4,5},{5,6},{6,7},{7,8},{8,9},{9,10},{10,1... | collective-permute-start | bytes 786440 | tf_op jit(solution)/shard_map/ppermute | solution.py:17
  20.7 2.7 %copy-start.1 = (bf16[528,256]{1,0:T(8,128)(2,1)}, bf16[528,256]{1,0:T(8,128)(2,1)S(1)}, u32[]{:S(2)}) copy-start(bf16[528,256]{1,0:T(8,128)(2,1)S(1)} %collective-permute-done.1.kv_ref) | copy-start | bytes 811012
  20.7 12.8 %collective-permute-start.2 = (bf16[528,256]{1,0:T(8,128)(2,1)S(1)}, bf16[528,256]{1,0:T(8,128)(2,1)S(1)}, u32[]{:S(2)}, u32[]{:S(2)}) collective-permute-start(bf16[528,256]{1,0:T(8,128)(2,1)S(1)} %collective-permute-done.1.kv_ref), channel_id=1, source_target_pairs={{0,1},{1,2},{2,3},{3,4},{4,5},{5,6},{6,7},{7,8},{8,9},{9,10},{10,1... | collective-permute-start | bytes 811016 | tf_op jit(solution)/shard_map/ppermute | solution.py:17
  23.2 9.1 %collective-permute-start.4 = (f32[512,128]{1,0:T(8,128)S(1)}, f32[512,128]{1,0:T(8,128)S(1)}, u32[]{:S(2)}, u32[]{:S(2)}) collective-permute-start(f32[512,128]{1,0:T(8,128)S(1)} %add.20), channel_id=1, source_target_pairs={{0,1},{1,2},{2,3},{3,4},{4,5},{5,6},{6,7},{7,8},{8,9},{9,10},{10,1... | collective-permute-start | bytes 786440 | tf_op jit(solution)/shard_map/ppermute | solution.py:17
  30.5 9.6 %collective-permute-start.9 = (f32[512,128]{1,0:T(8,128)S(1)}, f32[512,128]{1,0:T(8,128)S(1)}, u32[]{:S(2)}, u32[]{:S(2)}) collective-permute-start(f32[512,128]{1,0:T(8,128)S(1)} %add.24), channel_id=1, source_target_pairs={{0,1},{1,2},{2,3},{3,4},{4,5},{5,6},{6,7},{7,8},{8,9},{9,10},{10,1... | collective-permute-start | bytes 786440 | tf_op jit(solution)/shard_map/ppermute | solution.py:17
  33.3 24.9 %collective-permute-start.5 = (f32[512,128]{1,0:T(8,128)S(1)}, f32[512,128]{1,0:T(8,128)S(1)}, u32[]{:S(2)}, u32[]{:S(2)}) collective-permute-start(f32[512,128]{1,0:T(8,128)S(1)} %add.21), channel_id=1, source_target_pairs={{0,1},{1,2},{2,3},{3,4},{4,5},{5,6},{6,7},{7,8},{8,9},{9,10},{10,1... | collective-permute-start | bytes 786440 | tf_op jit(solution)/shard_map/ppermute | solution.py:17
  33.5 0.7 %copy-start.2 = (bf16[528,256]{1,0:T(8,128)(2,1)}, bf16[528,256]{1,0:T(8,128)(2,1)S(1)}, u32[]{:S(2)}) copy-start(bf16[528,256]{1,0:T(8,128)(2,1)S(1)} %collective-permute-done.2.kv_ref) | copy-start | bytes 811012
  41.1 19.6 %collective-permute-start.10 = (bf16[512,128]{1,0:T(8,128)(2,1)S(1)}, bf16[512,128]{1,0:T(8,128)(2,1)S(1)}, u32[]{:S(2)}, u32[]{:S(2)}) collective-permute-start(bf16[512,128]{1,0:T(8,128)(2,1)S(1)} %add_convert_fusion), channel_id=1, source_target_pairs={{0,253},{1,254},{2,255},{3,0},{4,1},{5,2},{6,3},{7,4},{8,5},{9,6},... | collective-permute-start | bytes 393224 | tf_op jit(solution)/shard_map/ppermute | solution.py:17
  59.2 4.5 %collective-permute-start.6 = (bf16[512,128]{1,0:T(8,128)(2,1)S(1)}, bf16[512,128]{1,0:T(8,128)(2,1)S(1)}, u32[]{:S(2)}, u32[]{:S(2)}) collective-permute-start(bf16[512,128]{1,0:T(8,128)(2,1)S(1)} %add_convert_fusion.1), channel_id=1, source_target_pairs={{0,253},{1,254},{2,255},{3,0},{4,1},{5,2},{6,3},{7,4},{8,5},{9,6},... | collective-permute-start | bytes 393224 | tf_op jit(solution)/shard_map/ppermute | solution.py:17

commit v2 on v1

--- a/solution.py
+++ b/solution.py
@@ -22,15 +22,14 @@
     if has_in:
         dqin_ref, *rest = rest
     if own:
-        dq_ref, dk_ref, dv_ref, dlo_ref, acc_ref = rest
+        dq_ref, dkv_ref, dlo_ref, acc_ref = rest
     else:
-        dq_ref, dk_ref, dv_ref, acc_ref = rest
+        dq_ref, dkv_ref, acc_ref = rest
     block = pl.program_id(0)
 
     @pl.when(block == 0)
     def _():
-        dk_ref[...] = jnp.zeros_like(dk_ref)
-        dv_ref[...] = jnp.zeros_like(dv_ref)
+        dkv_ref[...] = jnp.zeros_like(dkv_ref)
 
     if has_in:
         acc_ref[...] = dqin_ref[...]
@@ -96,8 +95,8 @@
 
         for j in range(group):
             add_to(acc_ref, pl.ds(j * width, width), dq[j * half:(j + 1) * half], q_sel)
-        add_to(dk_ref, pl.ds(0, width), dk, k_sel)
-        add_to(dv_ref, pl.ds(0, width), dv, k_sel)
+        add_to(dkv_ref, pl.ds(0, width), dk, k_sel)
+        add_to(dkv_ref, pl.ds(width, width), dv, k_sel)
     dq_ref[...] = acc_ref[...].astype(dq_ref.dtype)
 
 
@@ -114,7 +113,7 @@
     own = delta.shape == queries.shape
     col_spec = pl.BlockSpec((rows, GROUP * width), lambda g, info: (0, g))
     kv_spec = pl.BlockSpec(kv.shape, lambda g, info: (0, 0))
-    part_spec = pl.BlockSpec((rows, width), lambda g, info: (0, 0))
+    part_spec = pl.BlockSpec((rows, 2 * width), lambda g, info: (0, 0))
     row_spec = pl.BlockSpec((heads, rows), lambda g, info: (0, 0))
     group_spec = pl.BlockSpec((1, GROUP, rows), lambda g, info: (g, 0, 0))
     in_specs = [col_spec, col_spec, kv_spec, row_spec, col_spec if own else group_spec]
@@ -127,10 +126,9 @@
             aliases = {len(args): 0}
     out_shape = [
         jax.ShapeDtypeStruct((rows, cols), dq_dtype),
-        jax.ShapeDtypeStruct((rows, width), jnp.float32),
-        jax.ShapeDtypeStruct((rows, width), jnp.float32),
+        jax.ShapeDtypeStruct((rows, 2 * width), jnp.float32),
     ]
-    out_specs = [col_spec, part_spec, part_spec]
+    out_specs = [col_spec, part_spec]
     if own:
         out_shape.append(jax.ShapeDtypeStruct((heads // GROUP, GROUP, rows), jnp.float32))
         out_specs.append(group_spec)
@@ -169,21 +167,18 @@
         visitors.append(passed_along(visitors[-1], "ctx", 1))
 
     own_info = block_pair
-    dq, sum_k, sum_v, delta = tile_step(OWN_TILES, own_info, queries, grad_out, kv,
+    dq, sums, delta = tile_step(OWN_TILES, own_info, queries, grad_out, kv,
                                         log_total, attn_out, None, jnp.float32)
     for step in range(1, STEPS):
-        got_k = passed_along(sum_k, "ctx", 1)
-        got_v = passed_along(sum_v, "ctx", 1)
+        received = passed_along(sums, "ctx", 1)
         kv_s = visitors[step]
         last = step == STEPS - 1
-        dq, part_k, part_v = tile_step(VISIT_TILES, own_info, queries, grad_out, kv_s,
+        dq, part = tile_step(VISIT_TILES, own_info, queries, grad_out, kv_s,
                                        log_total, delta, dq,
                                        jnp.bfloat16 if last else jnp.float32)
-        sum_k = got_k + part_k
-        sum_v = got_v + part_v
-    final_k = passed_along(sum_k.astype(jnp.bfloat16), "ctx", 1 - STEPS)
-    final_v = passed_along(sum_v.astype(jnp.bfloat16), "ctx", 1 - STEPS)
-    return dq, final_k, final_v
+        sums = received + part
+    final = passed_along(sums.astype(jnp.bfloat16), "ctx", 1 - STEPS)
+    return dq, final[:, :width], final[:, width:]
 
 
 def solution(mesh):

time: 65.3 us -> 96.7 us (1.48)
  the two profiles are of different devices: /device:TPU:2 before, /device:TPU:125 now
where the time goes in v2:
time: 96.7 us; the launch traced here: 95 us
  waiting for transfers between devices  45.4 us (47%)
  Pallas kernels  26.3 us (27%)
  starting transfers between devices  14.1 us (15%)
  other arithmetic  5.03 us (5%)
  local copies, waits for them, and re-layouts  2.9 us (3%)
  between operations  1.31 us (1%)
    ppermute x7, waiting for transfers between devices, passed_along(): return lax.ppermute(value, axis, pairs)  45.4 us
    pallas_call x4, Pallas kernels, tile_step(): pl.pallas_call(functools.partial(tile_body, tiles, has_in, own, GROUP, ha...  26.3 us
    ppermute x7, starting transfers between devices, passed_along(): return lax.ppermute(value, axis, pairs)  14.1 us
    add x2, other arithmetic, device_steps(): sums = received + part  2.22 us
    unnamed x8, local copies, waits for them, and re-layouts  2.19 us
  transfers between devices with their start and end apart: 7, of which 4 were waited for; matrix products, arithmetic and copies ran while one was open for 0% of the time, Pallas kernels for 20%

profile of v2, /device:TPU:125, one launch (start us, length us, event | category | flops | bytes accessed | tf_op | source)
XLA Modules:
  0.0 95.0 jit_solution(3912464894687433134)
XLA Ops:
  1.3 1.7 %fusion.2.kv_ref = bf16[528,256]{1,0:T(8,128)(2,1)} fusion(bf16[512,128]{1,0:T(8,128)(2,1)} %param.9, bf16[512,128]{1,0:T(8,128)(2,1)} %param.8, bf16[]{:T(256)} %bitcast), kind=kLoop, calls=%fused_computation.4 | loop fusion | flops 946176 | bytes 532482 | tf_op jit(solution)/shard_map/concatenate | solution.py:163
  3.0 0.0 copy-start
  3.0 7.7 %shard_map.94 = (f32[512,1024]{1,0:T(8,128)}, f32[512,256]{1,0:T(8,128)}, f32[2,4,512]{2,1,0:T(4,128)}) custom-call(s32[1]{0:T(128)S(6)} %copy.14.info_ref, bf16[512,1024]{1,0:T(8,128)(2,1)} %q_ref.7, bf16[512,1024]{1,0:T(8,128)(2,1)} %do_ref.7, bf16[528,256]{1,0:T(8,128)(2,1)} %fusion.2.kv_ref, f32[8,512]{1,0:T(8,128)} %lse_ref.7, bf16[512,1024]{1,0:T(8,128)(2,1)} %dl_ref.1), custom_call_target="tpu_custom_call" | custom-call | flops 2013265920 | bytes 4456448 | tf_op jit(solution)/shard_map/pallas_call | solution.py:137
  10.7 1.5 %collective-permute-start.3 = (f32[512,256]{1,0:T(8,128)}, f32[512,256]{1,0:T(8,128)S(1)}, u32[]{:S(2)}, u32[]{:S(2)}) collective-permute-start(f32[512,256]{1,0:T(8,128)} %get-tuple-element.17), channel_id=1, source_target_pairs={{0,1},{1,2},{2,3},{3,4},{4,5},{5,6},{6,7},{7,8},{8,9},{9,10},{10,1... | collective-permute-start | bytes 1572872 | tf_op jit(solution)/shard_map/ppermute | solution.py:17
  12.2 0.0 copy-done
  12.2 0.1 collective-permute-start
  12.3 9.1 %collective-permute-done.kv_ref = bf16[528,256]{1,0:T(8,128)(2,1)S(1)} collective-permute-done((bf16[528,256]{1,0:T(8,128)(2,1)S(1)}, bf16[528,256]{1,0:T(8,128)(2,1)S(1)}, u32[]{:S(2)}, u32[]{:S(2)}) %collective-permute-start) | collective-permute-done | bytes 270368 | tf_op jit(solution)/shard_map/ppermute | solution.py:17
  21.4 0.0 copy-start.1
  21.4 0.7 copy-done.1
  22.1 6.3 %shard_map.95 = (f32[512,1024]{1,0:T(8,128)}, f32[512,256]{1,0:T(8,128)}) custom-call(s32[1]{0:T(128)S(6)} %copy.14.info_ref, bf16[512,1024]{1,0:T(8,128)(2,1)} %q_ref.7, bf16[512,1024]{1,0:T(8,128)(2,1)} %do_ref.7, bf16[528,256]{1,0:T(8,128)(2,1)} %copy-done.1, f32[8,512]{1,0:T(8,128)} %lse_ref.7, ...), custom_call_target="tpu_custom_call", output_to_operand_aliasing={{0}: (6, {})} | custom-call | flops 1342177280 | bytes 6553600 | tf_op jit(solution)/shard_map/pallas_call | solution.py:137
  28.4 0.0 collective-permute-done.3
  28.4 1.1 %add.11 = f32[512,256]{1,0:T(8,128)S(1)} add(f32[512,256]{1,0:T(8,128)S(1)} %collective-permute-done.3, f32[512,256]{1,0:T(8,128)} %get-tuple-element.18) | non-fusion elementwise | flops 131072 | bytes 1572864 | tf_op jit(solution)/shard_map/add | solution.py:179
  29.5 2.5 %collective-permute-start.4 = (f32[512,256]{1,0:T(8,128)S(1)}, f32[512,256]{1,0:T(8,128)S(1)}, u32[]{:S(2)}, u32[]{:S(2)}) collective-permute-start(f32[512,256]{1,0:T(8,128)S(1)} %add.11), channel_id=1, source_target_pairs={{0,1},{1,2},{2,3},{3,4},{4,5},{5,6},{6,7},{7,8},{8,9},{9,10},{10,1... | collective-permute-start | bytes 1572872 | tf_op jit(solution)/shard_map/ppermute | solution.py:17
  32.1 0.3 collective-permute-start.1
  32.4 8.8 %collective-permute-done.1.kv_ref = bf16[528,256]{1,0:T(8,128)(2,1)S(1)} collective-permute-done((bf16[528,256]{1,0:T(8,128)(2,1)}, bf16[528,256]{1,0:T(8,128)(2,1)S(1)}, u32[]{:S(2)}, u32[]{:S(2)}) %collective-permute-start.1) | collective-permute-done | bytes 270368 | tf_op jit(solution)/shard_map/ppermute | solution.py:17
  41.2 0.0 copy-start.2
  41.2 0.7 copy-done.2
  41.9 6.3 %shard_map.96 = (f32[512,1024]{1,0:T(8,128)}, f32[512,256]{1,0:T(8,128)}) custom-call(s32[1]{0:T(128)S(6)} %copy.14.info_ref, bf16[512,1024]{1,0:T(8,128)(2,1)} %q_ref.7, bf16[512,1024]{1,0:T(8,128)(2,1)} %do_ref.7, bf16[528,256]{1,0:T(8,128)(2,1)} %copy-done.2, f32[8,512]{1,0:T(8,128)} %lse_ref.7, ...), custom_call_target="tpu_custom_call", output_to_operand_aliasing={{0}: (6, {})} | custom-call | flops 1342177280 | bytes 6553600 | tf_op jit(solution)/shard_map/pallas_call | solution.py:137
  48.2 0.0 collective-permute-done.4
  48.2 1.1 %add.12 = f32[512,256]{1,0:T(8,128)S(1)} add(f32[512,256]{1,0:T(8,128)S(1)} %collective-permute-done.4, f32[512,256]{1,0:T(8,128)} %get-tuple-element.19) | non-fusion elementwise | flops 131072 | bytes 1572864 | tf_op jit(solution)/shard_map/add | solution.py:179
  49.3 2.5 %collective-permute-start.5 = (f32[512,256]{1,0:T(8,128)S(1)}, f32[512,256]{1,0:T(8,128)S(1)}, u32[]{:S(2)}, u32[]{:S(2)}) collective-permute-start(f32[512,256]{1,0:T(8,128)S(1)} %add.12), channel_id=1, source_target_pairs={{0,1},{1,2},{2,3},{3,4},{4,5},{5,6},{6,7},{7,8},{8,9},{9,10},{10,1... | collective-permute-start | bytes 1572872 | tf_op jit(solution)/shard_map/ppermute | solution.py:17
  51.8 5.9 %collective-permute-start.2 = (bf16[528,256]{1,0:T(8,128)(2,1)}, bf16[528,256]{1,0:T(8,128)(2,1)S(1)}, u32[]{:S(2)}, u32[]{:S(2)}) collective-permute-start(bf16[528,256]{1,0:T(8,128)(2,1)} %copy-done.2), channel_id=1, source_target_pairs={{0,1},{1,2},{2,3},{3,4},{4,5},{5,6},{6,7},{7,8},{8,9},{9,10},{10,1... | collective-permute-start | bytes 811016 | tf_op jit(solution)/shard_map/ppermute | solution.py:17
  57.6 3.7 %collective-permute-done.2.kv_ref = bf16[528,256]{1,0:T(8,128)(2,1)S(1)} collective-permute-done((bf16[528,256]{1,0:T(8,128)(2,1)}, bf16[528,256]{1,0:T(8,128)(2,1)S(1)}, u32[]{:S(2)}, u32[]{:S(2)}) %collective-permute-start.2) | collective-permute-done | bytes 270368 | tf_op jit(solution)/shard_map/ppermute | solution.py:17
  61.4 0.0 copy-start.3
  61.4 0.7 copy-done.3
  62.1 6.1 %shard_map.97 = (bf16[512,1024]{1,0:T(8,128)(2,1)}, f32[512,256]{1,0:T(8,128)}) custom-call(s32[1]{0:T(128)S(6)} %copy.14.info_ref, bf16[512,1024]{1,0:T(8,128)(2,1)} %q_ref.7, bf16[512,1024]{1,0:T(8,128)(2,1)} %do_ref.7, bf16[528,256]{1,0:T(8,128)(2,1)} %copy-done.3, f32[8,512]{1,0:T(8,128)} %lse_ref.7, f32[2,4,512]{2,1,0:T(4,128)} %get-tuple-element.12.dl_ref, ...), custom_call_target="tpu_custom_call" | custom-call | flops 1342177280 | bytes 6553600 | tf_op jit(solution)/shard_map/pallas_call | solution.py:137
  68.2 0.0 collective-permute-done.5
  68.2 1.1 %add_convert_fusion = bf16[512,256]{1,0:T(8,128)(2,1)S(1)} fusion(f32[512,256]{1,0:T(8,128)S(1)} %collective-permute-done.5, f32[512,256]{1,0:T(8,128)} %get-tuple-element.20), kind=kLoop, calls=%fused_computation.3 | loop fusion | flops 262144 | bytes 1310720 | tf_op jit(solution)/shard_map/convert_element_type | solution.py:180
  69.3 1.3 %collective-permute-start.6 = (bf16[512,256]{1,0:T(8,128)(2,1)S(1)}, bf16[512,256]{1,0:T(8,128)(2,1)S(1)}, u32[]{:S(2)}, u32[]{:S(2)}) collective-permute-start(bf16[512,256]{1,0:T(8,128)(2,1)S(1)} %add_convert_fusion), channel_id=1, source_target_pairs={{0,253},{1,254},{2,255},{3,0},{4,1},{5,2},{6,3},{7,4},{8,5},{9,6},... | collective-permute-start | bytes 786440 | tf_op jit(solution)/shard_map/ppermute | solution.py:17
  70.6 23.7 %collective-permute-done.6 = bf16[512,256]{1,0:T(8,128)(2,1)S(1)} collective-permute-done((bf16[512,256]{1,0:T(8,128)(2,1)S(1)}, bf16[512,256]{1,0:T(8,128)(2,1)S(1)}, u32[]{:S(2)}, u32[]{:S(2)}) %collective-permute-start.6) | collective-permute-done | bytes 262176 | tf_op jit(solution)/shard_map/ppermute | solution.py:17
  94.3 0.7 fusion.3
Async XLA Ops:
  3.0 9.2 %copy-start = (bf16[528,256]{1,0:T(8,128)(2,1)S(1)}, bf16[528,256]{1,0:T(8,128)(2,1)}, u32[]{:S(2)}) copy-start(bf16[528,256]{1,0:T(8,128)(2,1)} %fusion.2.kv_ref) | copy-start | bytes 811012
  10.7 17.7 %collective-permute-start.3 = (f32[512,256]{1,0:T(8,128)}, f32[512,256]{1,0:T(8,128)S(1)}, u32[]{:S(2)}, u32[]{:S(2)}) collective-permute-start(f32[512,256]{1,0:T(8,128)} %get-tuple-element.17), channel_id=1, source_target_pairs={{0,1},{1,2},{2,3},{3,4},{4,5},{5,6},{6,7},{7,8},{8,9},{9,10},{10,1... | collective-permute-start | bytes 1572872 | tf_op jit(solution)/shard_map/ppermute | solution.py:17
  12.2 9.2 %collective-permute-start = (bf16[528,256]{1,0:T(8,128)(2,1)S(1)}, bf16[528,256]{1,0:T(8,128)(2,1)S(1)}, u32[]{:S(2)}, u32[]{:S(2)}) collective-permute-start(bf16[528,256]{1,0:T(8,128)(2,1)S(1)} %copy-done), channel_id=1, source_target_pairs={{0,1},{1,2},{2,3},{3,4},{4,5},{5,6},{6,7},{7,8},{8,9},{9,10},{10,1... | collective-permute-start | bytes 811016 | tf_op jit(solution)/shard_map/ppermute | solution.py:17
  21.4 0.7 copy-start.1
  29.5 18.7 %collective-permute-start.4 = (f32[512,256]{1,0:T(8,128)S(1)}, f32[512,256]{1,0:T(8,128)S(1)}, u32[]{:S(2)}, u32[]{:S(2)}) collective-permute-start(f32[512,256]{1,0:T(8,128)S(1)} %add.11), channel_id=1, source_target_pairs={{0,1},{1,2},{2,3},{3,4},{4,5},{5,6},{6,7},{7,8},{8,9},{9,10},{10,1... | collective-permute-start | bytes 1572872 | tf_op jit(solution)/shard_map/ppermute | solution.py:17
  32.1 9.1 %collective-permute-start.1 = (bf16[528,256]{1,0:T(8,128)(2,1)}, bf16[528,256]{1,0:T(8,128)(2,1)S(1)}, u32[]{:S(2)}, u32[]{:S(2)}) collective-permute-start(bf16[528,256]{1,0:T(8,128)(2,1)} %copy-done.1), channel_id=1, source_target_pairs={{0,1},{1,2},{2,3},{3,4},{4,5},{5,6},{6,7},{7,8},{8,9},{9,10},{10,1... | collective-permute-start | bytes 811016 | tf_op jit(solution)/shard_map/ppermute | solution.py:17
  41.2 0.7 copy-start.2
  49.3 18.8 %collective-permute-start.5 = (f32[512,256]{1,0:T(8,128)S(1)}, f32[512,256]{1,0:T(8,128)S(1)}, u32[]{:S(2)}, u32[]{:S(2)}) collective-permute-start(f32[512,256]{1,0:T(8,128)S(1)} %add.12), channel_id=1, source_target_pairs={{0,1},{1,2},{2,3},{3,4},{4,5},{5,6},{6,7},{7,8},{8,9},{9,10},{10,1... | collective-permute-start | bytes 1572872 | tf_op jit(solution)/shard_map/ppermute | solution.py:17
  51.8 9.6 %collective-permute-start.2 = (bf16[528,256]{1,0:T(8,128)(2,1)}, bf16[528,256]{1,0:T(8,128)(2,1)S(1)}, u32[]{:S(2)}, u32[]{:S(2)}) collective-permute-start(bf16[528,256]{1,0:T(8,128)(2,1)} %copy-done.2), channel_id=1, source_target_pairs={{0,1},{1,2},{2,3},{3,4},{4,5},{5,6},{6,7},{7,8},{8,9},{9,10},{10,1... | collective-permute-start | bytes 811016 | tf_op jit(solution)/shard_map/ppermute | solution.py:17
  61.4 0.7 copy-start.3
  69.3 25.0 %collective-permute-start.6 = (bf16[512,256]{1,0:T(8,128)(2,1)S(1)}, bf16[512,256]{1,0:T(8,128)(2,1)S(1)}, u32[]{:S(2)}, u32[]{:S(2)}) collective-permute-start(bf16[512,256]{1,0:T(8,128)(2,1)S(1)} %add_convert_fusion), channel_id=1, source_target_pairs={{0,253},{1,254},{2,255},{3,0},{4,1},{5,2},{6,3},{7,4},{8,5},{9,6},... | collective-permute-start | bytes 786440 | tf_op jit(solution)/shard_map/ppermute | solution.py:17

commit v3 on v2

--- a/solution.py
+++ b/solution.py
@@ -54,28 +54,47 @@
         mine = jnp.full((1, 2 * width), info_ref[0], jnp.int32).astype(jnp.float32)
         upper = (seen > mine)[:, 0:1]
     lo_rows, hi_rows = pl.ds(0, half), pl.ds(half, half)
-    for q_sel, k_sel, diag in tiles:
+    for q_sel, k_sel, diag, qo, ql, ko, kl in tiles:
         def pick(hi, lo, sel=q_sel):
             if sel is None:
                 return jnp.where(upper, hi, lo)
             return hi if sel == 1 else lo
 
-        lse = jnp.concatenate([pick(x[:, half:], x[:, :half]) for x in lse_all], axis=1)
-        dl = jnp.concatenate([pick(x[:, half:], x[:, :half]) for x in dl_all], axis=1)
-        q = jnp.concatenate(
-            [pick(q_ref[hi_rows, pl.ds(j * width, width)], q_ref[lo_rows, pl.ds(j * width, width)])
-             for j in range(group)], axis=0)
-        do = jnp.concatenate(
-            [pick(do_ref[hi_rows, pl.ds(j * width, width)], do_ref[lo_rows, pl.ds(j * width, width)])
-             for j in range(group)], axis=0)
-        k = pick(kv_ref[hi_rows, pl.ds(0, width)], kv_ref[lo_rows, pl.ds(0, width)], k_sel)
-        v = pick(kv_ref[hi_rows, pl.ds(width, width)], kv_ref[lo_rows, pl.ds(width, width)], k_sel)
+        def q_slice(sel, start, length):
+            return pl.ds((sel or 0) * half + start, length)
+
+        if q_sel is None:
+            lse = jnp.concatenate([pick(x[:, half:], x[:, :half]) for x in lse_all], axis=1)
+            dl = jnp.concatenate([pick(x[:, half:], x[:, :half]) for x in dl_all], axis=1)
+            q = jnp.concatenate(
+                [pick(q_ref[hi_rows, pl.ds(j * width, width)],
+                      q_ref[lo_rows, pl.ds(j * width, width)]) for j in range(group)], axis=0)
+            do = jnp.concatenate(
+                [pick(do_ref[hi_rows, pl.ds(j * width, width)],
+                      do_ref[lo_rows, pl.ds(j * width, width)]) for j in range(group)], axis=0)
+        else:
+            lanes = slice(q_sel * half + qo, q_sel * half + qo + ql)
+            lse = jnp.concatenate([x[:, lanes] for x in lse_all], axis=1)
+            dl = jnp.concatenate([x[:, lanes] for x in dl_all], axis=1)
+            rows_q = q_slice(q_sel, qo, ql)
+            q = jnp.concatenate(
+                [q_ref[rows_q, pl.ds(j * width, width)] for j in range(group)], axis=0)
+            do = jnp.concatenate(
+                [do_ref[rows_q, pl.ds(j * width, width)] for j in range(group)], axis=0)
+        if k_sel is None:
+            k = pick(kv_ref[hi_rows, pl.ds(0, width)], kv_ref[lo_rows, pl.ds(0, width)], k_sel)
+            v = pick(kv_ref[hi_rows, pl.ds(width, width)], kv_ref[lo_rows, pl.ds(width, width)],
+                     k_sel)
+        else:
+            rows_k = q_slice(k_sel, ko, kl)
+            k = kv_ref[rows_k, pl.ds(0, width)]
+            v = kv_ref[rows_k, pl.ds(width, width)]
         s_t = lax.dot_general(k, q, (((1,), (1,)), ((), ())),
                               preferred_element_type=jnp.float32) * scale
         p_t = jnp.exp(s_t - lse)
         if diag:
-            rows = lax.broadcasted_iota(jnp.int32, (half, group * half), 0)
-            cols_i = lax.broadcasted_iota(jnp.int32, (half, group * half), 1) % half
+            rows = lax.broadcasted_iota(jnp.int32, (kl, group * ql), 0) + ko
+            cols_i = lax.broadcasted_iota(jnp.int32, (kl, group * ql), 1) % ql + qo
             p_t = jnp.where(rows <= cols_i, p_t, 0.0)
         dp_t = lax.dot_general(v, do, (((1,), (1,)), ((), ())),
                                preferred_element_type=jnp.float32)
@@ -86,17 +105,17 @@
         dq = lax.dot_general(ds_t, k, (((0,), (0,)), ((), ())),
                              preferred_element_type=jnp.float32)
 
-        def add_to(ref, cols, value, sel):
+        def add_to(ref, cols, value, sel, start, length):
             if sel is None:
                 ref[hi_rows, cols] += jnp.where(upper, value, 0.0)
                 ref[lo_rows, cols] += jnp.where(upper, 0.0, value)
             else:
-                ref[hi_rows if sel == 1 else lo_rows, cols] += value
+                ref[q_slice(sel, start, length), cols] += value
 
         for j in range(group):
-            add_to(acc_ref, pl.ds(j * width, width), dq[j * half:(j + 1) * half], q_sel)
-        add_to(dkv_ref, pl.ds(0, width), dk, k_sel)
-        add_to(dkv_ref, pl.ds(width, width), dv, k_sel)
+            add_to(acc_ref, pl.ds(j * width, width), dq[j * ql:(j + 1) * ql], q_sel, qo, ql)
+        add_to(dkv_ref, pl.ds(0, width), dk, k_sel, ko, kl)
+        add_to(dkv_ref, pl.ds(width, width), dv, k_sel, ko, kl)
     dq_ref[...] = acc_ref[...].astype(dq_ref.dtype)
 
 
@@ -132,7 +151,7 @@
     if own:
         out_shape.append(jax.ShapeDtypeStruct((heads // GROUP, GROUP, rows), jnp.float32))
         out_specs.append(group_spec)
-    flops = len(tiles) * heads * 5 * 2 * half * half * width
+    flops = sum(t[4] * t[6] for t in tiles) * heads * 5 * 2 * width
     nbytes = 2 * rows * cols * 2 + rows * 2 * width * 2 + rows * cols * 4 * (2 if has_in else 1)
     return pl.pallas_call(
         functools.partial(tile_body, tiles, has_in, own, GROUP, half, width, scale),
@@ -147,13 +166,17 @@
         input_output_aliases=aliases,
         compiler_params=pltpu.CompilerParams(dimension_semantics=("arbitrary",)),
         cost_estimate=pl.CostEstimate(
-            flops=flops, transcendentals=len(tiles) * heads * half * half, bytes_accessed=nbytes
+            flops=flops, transcendentals=sum(t[4] * t[6] for t in tiles) * heads, bytes_accessed=nbytes
         ),
     )(info, *args)
 
 
-OWN_TILES = ((0, 0, True), (1, 0, False), (1, 1, True))
-VISIT_TILES = ((1, 0, False), (None, None, False))
+OWN_TILES = (
+    (0, 0, True, 0, 256, 0, 128), (0, 0, True, 128, 128, 128, 128),
+    (1, 0, False, 0, 256, 0, 256),
+    (1, 1, True, 0, 256, 0, 128), (1, 1, True, 128, 128, 128, 128),
+)
+VISIT_TILES = ((1, 0, False, 0, 256, 0, 256), (None, None, False, 0, 256, 0, 256))
 
 
 def device_steps(queries, key_rows, value_rows, grad_out, attn_out, log_total, block_pair):

time: 96.7 us -> 96.4 us (level)
  no operation moved by 1% of the time
where the time goes in v3:
time: 96.4 us; the launch traced here: 94.6 us
  waiting for transfers between devices  45.4 us (47%)
  Pallas kernels  25.9 us (27%)
  starting transfers between devices  14.1 us (15%)
  other arithmetic  5.03 us (5%)
  local copies, waits for them, and re-layouts  2.9 us (3%)
  between operations  1.31 us (1%)
    ppermute x7, waiting for transfers between devices, passed_along(): return lax.ppermute(value, axis, pairs)  45.4 us
    pallas_call x4, Pallas kernels, tile_step(): pl.pallas_call(functools.partial(tile_body, tiles, has_in, own, GROUP, ha...  25.9 us
    ppermute x7, starting transfers between devices, passed_along(): return lax.ppermute(value, axis, pairs)  14.1 us
    add x2, other arithmetic, device_steps(): sums = received + part  2.22 us
    unnamed x8, local copies, waits for them, and re-layouts  2.19 us
  transfers between devices with their start and end apart: 7, of which 4 were waited for; matrix products, arithmetic and copies ran while one was open for 0% of the time, Pallas kernels for 20%

profile of v3, /device:TPU:125, one launch (start us, length us, event | category | flops | bytes accessed | tf_op | source)
XLA Modules:
  0.0 94.6 jit_solution(15799810736199818213)
XLA Ops:
  1.3 1.7 %fusion.2.kv_ref = bf16[528,256]{1,0:T(8,128)(2,1)} fusion(bf16[512,128]{1,0:T(8,128)(2,1)} %param.9, bf16[512,128]{1,0:T(8,128)(2,1)} %param.8, bf16[]{:T(256)} %bitcast), kind=kLoop, calls=%fused_computation.4 | loop fusion | flops 946176 | bytes 532482 | tf_op jit(solution)/shard_map/concatenate | solution.py:186
  3.0 0.0 copy-start
  3.0 7.3 %shard_map.94 = (f32[512,1024]{1,0:T(8,128)}, f32[512,256]{1,0:T(8,128)}, f32[2,4,512]{2,1,0:T(4,128)}) custom-call(s32[1]{0:T(128)S(6)} %copy.14.info_ref, bf16[512,1024]{1,0:T(8,128)(2,1)} %q_ref.7, bf16[512,1024]{1,0:T(8,128)(2,1)} %do_ref.7, bf16[528,256]{1,0:T(8,128)(2,1)} %fusion.2.kv_ref, f32[8,512]{1,0:T(8,128)} %lse_ref.7, bf16[512,1024]{1,0:T(8,128)(2,1)} %dl_ref.1), custom_call_target="tpu_custom_call" | custom-call | flops 1677721600 | bytes 4456448 | tf_op jit(solution)/shard_map/pallas_call | solution.py:156
  10.3 1.5 %collective-permute-start.3 = (f32[512,256]{1,0:T(8,128)}, f32[512,256]{1,0:T(8,128)S(1)}, u32[]{:S(2)}, u32[]{:S(2)}) collective-permute-start(f32[512,256]{1,0:T(8,128)} %get-tuple-element.17), channel_id=1, source_target_pairs={{0,1},{1,2},{2,3},{3,4},{4,5},{5,6},{6,7},{7,8},{8,9},{9,10},{10,1... | collective-permute-start | bytes 1572872 | tf_op jit(solution)/shard_map/ppermute | solution.py:17
  11.8 0.0 copy-done
  11.8 0.1 collective-permute-start
  11.9 9.1 %collective-permute-done.kv_ref = bf16[528,256]{1,0:T(8,128)(2,1)S(1)} collective-permute-done((bf16[528,256]{1,0:T(8,128)(2,1)S(1)}, bf16[528,256]{1,0:T(8,128)(2,1)S(1)}, u32[]{:S(2)}, u32[]{:S(2)}) %collective-permute-start) | collective-permute-done | bytes 270368 | tf_op jit(solution)/shard_map/ppermute | solution.py:17
  21.0 0.0 copy-start.1
  21.0 0.7 copy-done.1
  21.8 6.3 %shard_map.95 = (f32[512,1024]{1,0:T(8,128)}, f32[512,256]{1,0:T(8,128)}) custom-call(s32[1]{0:T(128)S(6)} %copy.14.info_ref, bf16[512,1024]{1,0:T(8,128)(2,1)} %q_ref.7, bf16[512,1024]{1,0:T(8,128)(2,1)} %do_ref.7, bf16[528,256]{1,0:T(8,128)(2,1)} %copy-done.1, f32[8,512]{1,0:T(8,128)} %lse_ref.7, ...), custom_call_target="tpu_custom_call", output_to_operand_aliasing={{0}: (6, {})} | custom-call | flops 1342177280 | bytes 6553600 | tf_op jit(solution)/shard_map/pallas_call | solution.py:156
  28.0 0.0 collective-permute-done.3
  28.0 1.1 %add.11 = f32[512,256]{1,0:T(8,128)S(1)} add(f32[512,256]{1,0:T(8,128)S(1)} %collective-permute-done.3, f32[512,256]{1,0:T(8,128)} %get-tuple-element.18) | non-fusion elementwise | flops 131072 | bytes 1572864 | tf_op jit(solution)/shard_map/add | solution.py:202
  29.1 2.6 %collective-permute-start.4 = (f32[512,256]{1,0:T(8,128)S(1)}, f32[512,256]{1,0:T(8,128)S(1)}, u32[]{:S(2)}, u32[]{:S(2)}) collective-permute-start(f32[512,256]{1,0:T(8,128)S(1)} %add.11), channel_id=1, source_target_pairs={{0,1},{1,2},{2,3},{3,4},{4,5},{5,6},{6,7},{7,8},{8,9},{9,10},{10,1... | collective-permute-start | bytes 1572872 | tf_op jit(solution)/shard_map/ppermute | solution.py:17
  31.7 0.3 collective-permute-start.1
  32.0 8.8 %collective-permute-done.1.kv_ref = bf16[528,256]{1,0:T(8,128)(2,1)S(1)} collective-permute-done((bf16[528,256]{1,0:T(8,128)(2,1)}, bf16[528,256]{1,0:T(8,128)(2,1)S(1)}, u32[]{:S(2)}, u32[]{:S(2)}) %collective-permute-start.1) | collective-permute-done | bytes 270368 | tf_op jit(solution)/shard_map/ppermute | solution.py:17
  40.8 0.0 copy-start.2
  40.8 0.7 copy-done.2
  41.6 6.3 %shard_map.96 = (f32[512,1024]{1,0:T(8,128)}, f32[512,256]{1,0:T(8,128)}) custom-call(s32[1]{0:T(128)S(6)} %copy.14.info_ref, bf16[512,1024]{1,0:T(8,128)(2,1)} %q_ref.7, bf16[512,1024]{1,0:T(8,128)(2,1)} %do_ref.7, bf16[528,256]{1,0:T(8,128)(2,1)} %copy-done.2, f32[8,512]{1,0:T(8,128)} %lse_ref.7, ...), custom_call_target="tpu_custom_call", output_to_operand_aliasing={{0}: (6, {})} | custom-call | flops 1342177280 | bytes 6553600 | tf_op jit(solution)/shard_map/pallas_call | solution.py:156
  47.8 0.0 collective-permute-done.4
  47.8 1.1 %add.12 = f32[512,256]{1,0:T(8,128)S(1)} add(f32[512,256]{1,0:T(8,128)S(1)} %collective-permute-done.4, f32[512,256]{1,0:T(8,128)} %get-tuple-element.19) | non-fusion elementwise | flops 131072 | bytes 1572864 | tf_op jit(solution)/shard_map/add | solution.py:202
  48.9 2.5 %collective-permute-start.5 = (f32[512,256]{1,0:T(8,128)S(1)}, f32[512,256]{1,0:T(8,128)S(1)}, u32[]{:S(2)}, u32[]{:S(2)}) collective-permute-start(f32[512,256]{1,0:T(8,128)S(1)} %add.12), channel_id=1, source_target_pairs={{0,1},{1,2},{2,3},{3,4},{4,5},{5,6},{6,7},{7,8},{8,9},{9,10},{10,1... | collective-permute-start | bytes 1572872 | tf_op jit(solution)/shard_map/ppermute | solution.py:17
  51.4 5.9 %collective-permute-start.2 = (bf16[528,256]{1,0:T(8,128)(2,1)}, bf16[528,256]{1,0:T(8,128)(2,1)S(1)}, u32[]{:S(2)}, u32[]{:S(2)}) collective-permute-start(bf16[528,256]{1,0:T(8,128)(2,1)} %copy-done.2), channel_id=1, source_target_pairs={{0,1},{1,2},{2,3},{3,4},{4,5},{5,6},{6,7},{7,8},{8,9},{9,10},{10,1... | collective-permute-start | bytes 811016 | tf_op jit(solution)/shard_map/ppermute | solution.py:17
  57.3 3.7 %collective-permute-done.2.kv_ref = bf16[528,256]{1,0:T(8,128)(2,1)S(1)} collective-permute-done((bf16[528,256]{1,0:T(8,128)(2,1)}, bf16[528,256]{1,0:T(8,128)(2,1)S(1)}, u32[]{:S(2)}, u32[]{:S(2)}) %collective-permute-start.2) | collective-permute-done | bytes 270368 | tf_op jit(solution)/shard_map/ppermute | solution.py:17
  61.0 0.0 copy-start.3
  61.0 0.7 copy-done.3
  61.7 6.1 %shard_map.97 = (bf16[512,1024]{1,0:T(8,128)(2,1)}, f32[512,256]{1,0:T(8,128)}) custom-call(s32[1]{0:T(128)S(6)} %copy.14.info_ref, bf16[512,1024]{1,0:T(8,128)(2,1)} %q_ref.7, bf16[512,1024]{1,0:T(8,128)(2,1)} %do_ref.7, bf16[528,256]{1,0:T(8,128)(2,1)} %copy-done.3, f32[8,512]{1,0:T(8,128)} %lse_ref.7, f32[2,4,512]{2,1,0:T(4,128)} %get-tuple-element.12.dl_ref, ...), custom_call_target="tpu_custom_call" | custom-call | flops 1342177280 | bytes 6553600 | tf_op jit(solution)/shard_map/pallas_call | solution.py:156
  67.8 0.0 collective-permute-done.5
  67.8 1.1 %add_convert_fusion = bf16[512,256]{1,0:T(8,128)(2,1)S(1)} fusion(f32[512,256]{1,0:T(8,128)S(1)} %collective-permute-done.5, f32[512,256]{1,0:T(8,128)} %get-tuple-element.20), kind=kLoop, calls=%fused_computation.3 | loop fusion | flops 262144 | bytes 1310720 | tf_op jit(solution)/shard_map/convert_element_type | solution.py:203
  68.9 1.3 %collective-permute-start.6 = (bf16[512,256]{1,0:T(8,128)(2,1)S(1)}, bf16[512,256]{1,0:T(8,128)(2,1)S(1)}, u32[]{:S(2)}, u32[]{:S(2)}) collective-permute-start(bf16[512,256]{1,0:T(8,128)(2,1)S(1)} %add_convert_fusion), channel_id=1, source_target_pairs={{0,253},{1,254},{2,255},{3,0},{4,1},{5,2},{6,3},{7,4},{8,5},{9,6},... | collective-permute-start | bytes 786440 | tf_op jit(solution)/shard_map/ppermute | solution.py:17
  70.2 23.7 %collective-permute-done.6 = bf16[512,256]{1,0:T(8,128)(2,1)S(1)} collective-permute-done((bf16[512,256]{1,0:T(8,128)(2,1)S(1)}, bf16[512,256]{1,0:T(8,128)(2,1)S(1)}, u32[]{:S(2)}, u32[]{:S(2)}) %collective-permute-start.6) | collective-permute-done | bytes 262176 | tf_op jit(solution)/shard_map/ppermute | solution.py:17
  93.9 0.7 fusion.3
Async XLA Ops:
  3.0 8.8 %copy-start = (bf16[528,256]{1,0:T(8,128)(2,1)S(1)}, bf16[528,256]{1,0:T(8,128)(2,1)}, u32[]{:S(2)}) copy-start(bf16[528,256]{1,0:T(8,128)(2,1)} %fusion.2.kv_ref) | copy-start | bytes 811012
  10.3 17.7 %collective-permute-start.3 = (f32[512,256]{1,0:T(8,128)}, f32[512,256]{1,0:T(8,128)S(1)}, u32[]{:S(2)}, u32[]{:S(2)}) collective-permute-start(f32[512,256]{1,0:T(8,128)} %get-tuple-element.17), channel_id=1, source_target_pairs={{0,1},{1,2},{2,3},{3,4},{4,5},{5,6},{6,7},{7,8},{8,9},{9,10},{10,1... | collective-permute-start | bytes 1572872 | tf_op jit(solution)/shard_map/ppermute | solution.py:17
  11.8 9.2 %collective-permute-start = (bf16[528,256]{1,0:T(8,128)(2,1)S(1)}, bf16[528,256]{1,0:T(8,128)(2,1)S(1)}, u32[]{:S(2)}, u32[]{:S(2)}) collective-permute-start(bf16[528,256]{1,0:T(8,128)(2,1)S(1)} %copy-done), channel_id=1, source_target_pairs={{0,1},{1,2},{2,3},{3,4},{4,5},{5,6},{6,7},{7,8},{8,9},{9,10},{10,1... | collective-permute-start | bytes 811016 | tf_op jit(solution)/shard_map/ppermute | solution.py:17
  21.0 0.7 copy-start.1
  29.1 18.7 %collective-permute-start.4 = (f32[512,256]{1,0:T(8,128)S(1)}, f32[512,256]{1,0:T(8,128)S(1)}, u32[]{:S(2)}, u32[]{:S(2)}) collective-permute-start(f32[512,256]{1,0:T(8,128)S(1)} %add.11), channel_id=1, source_target_pairs={{0,1},{1,2},{2,3},{3,4},{4,5},{5,6},{6,7},{7,8},{8,9},{9,10},{10,1... | collective-permute-start | bytes 1572872 | tf_op jit(solution)/shard_map/ppermute | solution.py:17
  31.7 9.1 %collective-permute-start.1 = (bf16[528,256]{1,0:T(8,128)(2,1)}, bf16[528,256]{1,0:T(8,128)(2,1)S(1)}, u32[]{:S(2)}, u32[]{:S(2)}) collective-permute-start(bf16[528,256]{1,0:T(8,128)(2,1)} %copy-done.1), channel_id=1, source_target_pairs={{0,1},{1,2},{2,3},{3,4},{4,5},{5,6},{6,7},{7,8},{8,9},{9,10},{10,1... | collective-permute-start | bytes 811016 | tf_op jit(solution)/shard_map/ppermute | solution.py:17
  40.8 0.7 copy-start.2
  48.9 18.8 %collective-permute-start.5 = (f32[512,256]{1,0:T(8,128)S(1)}, f32[512,256]{1,0:T(8,128)S(1)}, u32[]{:S(2)}, u32[]{:S(2)}) collective-permute-start(f32[512,256]{1,0:T(8,128)S(1)} %add.12), channel_id=1, source_target_pairs={{0,1},{1,2},{2,3},{3,4},{4,5},{5,6},{6,7},{7,8},{8,9},{9,10},{10,1... | collective-permute-start | bytes 1572872 | tf_op jit(solution)/shard_map/ppermute | solution.py:17
  51.4 9.6 %collective-permute-start.2 = (bf16[528,256]{1,0:T(8,128)(2,1)}, bf16[528,256]{1,0:T(8,128)(2,1)S(1)}, u32[]{:S(2)}, u32[]{:S(2)}) collective-permute-start(bf16[528,256]{1,0:T(8,128)(2,1)} %copy-done.2), channel_id=1, source_target_pairs={{0,1},{1,2},{2,3},{3,4},{4,5},{5,6},{6,7},{7,8},{8,9},{9,10},{10,1... | collective-permute-start | bytes 811016 | tf_op jit(solution)/shard_map/ppermute | solution.py:17
  61.0 0.7 copy-start.3
  68.9 25.0 %collective-permute-start.6 = (bf16[512,256]{1,0:T(8,128)(2,1)S(1)}, bf16[512,256]{1,0:T(8,128)(2,1)S(1)}, u32[]{:S(2)}, u32[]{:S(2)}) collective-permute-start(bf16[512,256]{1,0:T(8,128)(2,1)S(1)} %add_convert_fusion), channel_id=1, source_target_pairs={{0,253},{1,254},{2,255},{3,0},{4,1},{5,2},{6,3},{7,4},{8,5},{9,6},... | collective-permute-start | bytes 786440 | tf_op jit(solution)/shard_map/ppermute | solution.py:17

commit v4 on v3

--- a/solution.py
+++ b/solution.py
@@ -130,11 +130,14 @@
     scale = width ** (-0.5)
     has_in = dq_in is not None
     own = delta.shape == queries.shape
-    col_spec = pl.BlockSpec((rows, GROUP * width), lambda g, info: (0, g))
+    group = GROUP if own else heads
+    if not own:
+        delta = delta.reshape(heads // group, group, rows)
+    col_spec = pl.BlockSpec((rows, group * width), lambda g, info: (0, g))
     kv_spec = pl.BlockSpec(kv.shape, lambda g, info: (0, 0))
     part_spec = pl.BlockSpec((rows, 2 * width), lambda g, info: (0, 0))
     row_spec = pl.BlockSpec((heads, rows), lambda g, info: (0, 0))
-    group_spec = pl.BlockSpec((1, GROUP, rows), lambda g, info: (g, 0, 0))
+    group_spec = pl.BlockSpec((1, group, rows), lambda g, info: (g, 0, 0))
     in_specs = [col_spec, col_spec, kv_spec, row_spec, col_spec if own else group_spec]
     args = [queries, grad_out, kv, lse, delta]
     aliases = {}
@@ -154,14 +157,14 @@
     flops = sum(t[4] * t[6] for t in tiles) * heads * 5 * 2 * width
     nbytes = 2 * rows * cols * 2 + rows * 2 * width * 2 + rows * cols * 4 * (2 if has_in else 1)
     return pl.pallas_call(
-        functools.partial(tile_body, tiles, has_in, own, GROUP, half, width, scale),
+        functools.partial(tile_body, tiles, has_in, own, group, half, width, scale),
         out_shape=tuple(out_shape),
         grid_spec=pltpu.PrefetchScalarGridSpec(
             num_scalar_prefetch=1,
-            grid=(heads // GROUP,),
+            grid=(heads // group,),
             in_specs=in_specs,
             out_specs=out_specs,
-            scratch_shapes=[pltpu.VMEM((rows, GROUP * width), jnp.float32)],
+            scratch_shapes=[pltpu.VMEM((rows, group * width), jnp.float32)],
         ),
         input_output_aliases=aliases,
         compiler_params=pltpu.CompilerParams(dimension_semantics=("arbitrary",)),

time: 96.4 us -> 98.5 us (1.022)
  the two profiles are of different devices: /device:TPU:125 before, /device:TPU:3 now
where the time goes in v4:
time: 98.5 us; the launch traced here: 98.2 us
  starting transfers between devices  30.3 us (31%)
  waiting for transfers between devices  29 us (29%)
  Pallas kernels  28.3 us (29%)
  other arithmetic  5.03 us (5%)
  local copies, waits for them, and re-layouts  4.23 us (4%)
  between operations  1.31 us (1%)
    ppermute x7, starting transfers between devices, passed_along(): return lax.ppermute(value, axis, pairs)  30.3 us
    ppermute x7, waiting for transfers between devices, passed_along(): return lax.ppermute(value, axis, pairs)  29 us
    pallas_call x4, Pallas kernels, tile_step(): pl.pallas_call(functools.partial(tile_body, tiles, has_in, own, group, ha...  28.3 us
    add x2, other arithmetic, device_steps(): sums = received + part  2.22 us
    unnamed x8, local copies, waits for them, and re-layouts  2.19 us
  transfers between devices with their start and end apart: 7, of which 4 were waited for; matrix products, arithmetic and copies ran while one was open for 1% of the time, Pallas kernels for 21%

profile of v4, /device:TPU:3, one launch (start us, length us, event | category | flops | bytes accessed | tf_op | source)
XLA Modules:
  0.0 98.2 jit_solution(12220285260913761116)
XLA Ops:
  1.3 1.7 %fusion.2.kv_ref = bf16[528,256]{1,0:T(8,128)(2,1)} fusion(bf16[512,128]{1,0:T(8,128)(2,1)} %param.9, bf16[512,128]{1,0:T(8,128)(2,1)} %param.8, bf16[]{:T(256)} %bitcast), kind=kLoop, calls=%fused_computation.4 | loop fusion | flops 946176 | bytes 532482 | tf_op jit(solution)/shard_map/concatenate | solution.py:189
  3.0 0.0 copy-start
  3.0 7.3 %shard_map.94 = (f32[512,1024]{1,0:T(8,128)}, f32[512,256]{1,0:T(8,128)}, f32[2,4,512]{2,1,0:T(4,128)}) custom-call(s32[1]{0:T(128)S(6)} %copy.14.info_ref, bf16[512,1024]{1,0:T(8,128)(2,1)} %q_ref.7, bf16[512,1024]{1,0:T(8,128)(2,1)} %do_ref.7, bf16[528,256]{1,0:T(8,128)(2,1)} %fusion.2.kv_ref, f32[8,512]{1,0:T(8,128)} %lse_ref.7, bf16[512,1024]{1,0:T(8,128)(2,1)} %dl_ref.1), custom_call_target="tpu_custom_call" | custom-call | flops 1677721600 | bytes 4456448 | tf_op jit(solution)/shard_map/pallas_call | solution.py:159
  10.3 1.8 %collective-permute-start.3 = (f32[512,256]{1,0:T(8,128)}, f32[512,256]{1,0:T(8,128)S(1)}, u32[]{:S(2)}, u32[]{:S(2)}) collective-permute-start(f32[512,256]{1,0:T(8,128)} %get-tuple-element.17), channel_id=1, source_target_pairs={{0,1},{1,2},{2,3},{3,4},{4,5},{5,6},{6,7},{7,8},{8,9},{9,10},{10,1... | collective-permute-start | bytes 1572872 | tf_op jit(solution)/shard_map/ppermute | solution.py:17
  12.1 0.0 copy-done
  12.1 0.1 collective-permute-start
  12.2 1.3 %reshape.12.dl_ref = f32[1,8,512]{2,1,0:T(8,128)} reshape(f32[2,4,512]{2,1,0:T(4,128)} %get-tuple-element.12) | data formatting | bytes 32768 | tf_op jit(solution)/shard_map/reshape | solution.py:135
  13.5 7.8 %collective-permute-done.kv_ref = bf16[528,256]{1,0:T(8,128)(2,1)S(1)} collective-permute-done((bf16[528,256]{1,0:T(8,128)(2,1)S(1)}, bf16[528,256]{1,0:T(8,128)(2,1)S(1)}, u32[]{:S(2)}, u32[]{:S(2)}) %collective-permute-start) | collective-permute-done | bytes 270368 | tf_op jit(solution)/shard_map/ppermute | solution.py:17
  21.3 0.0 copy-start.1
  21.3 0.7 copy-done.1
  22.0 7.1 %shard_map.95 = (f32[512,1024]{1,0:T(8,128)}, f32[512,256]{1,0:T(8,128)}) custom-call(s32[1]{0:T(128)S(6)} %copy.14.info_ref, bf16[512,1024]{1,0:T(8,128)(2,1)} %q_ref.7, bf16[512,1024]{1,0:T(8,128)(2,1)} %do_ref.7, bf16[528,256]{1,0:T(8,128)(2,1)} %copy-done.1, f32[8,512]{1,0:T(8,128)} %lse_ref.7, ...), custom_call_target="tpu_custom_call", output_to_operand_aliasing={{0}: (6, {})} | custom-call | flops 1342177280 | bytes 6553600 | tf_op jit(solution)/shard_map/pallas_call | solution.py:159
  29.2 0.0 collective-permute-done.3
  29.2 1.1 %add.11 = f32[512,256]{1,0:T(8,128)S(1)} add(f32[512,256]{1,0:T(8,128)S(1)} %collective-permute-done.3, f32[512,256]{1,0:T(8,128)} %get-tuple-element.18) | non-fusion elementwise | flops 131072 | bytes 1572864 | tf_op jit(solution)/shard_map/add | solution.py:205
  30.3 2.6 %collective-permute-start.4 = (f32[512,256]{1,0:T(8,128)S(1)}, f32[512,256]{1,0:T(8,128)S(1)}, u32[]{:S(2)}, u32[]{:S(2)}) collective-permute-start(f32[512,256]{1,0:T(8,128)S(1)} %add.11), channel_id=1, source_target_pairs={{0,1},{1,2},{2,3},{3,4},{4,5},{5,6},{6,7},{7,8},{8,9},{9,10},{10,1... | collective-permute-start | bytes 1572872 | tf_op jit(solution)/shard_map/ppermute | solution.py:17
  32.9 0.3 collective-permute-start.1
  33.1 8.9 %collective-permute-done.1.kv_ref = bf16[528,256]{1,0:T(8,128)(2,1)S(1)} collective-permute-done((bf16[528,256]{1,0:T(8,128)(2,1)}, bf16[528,256]{1,0:T(8,128)(2,1)S(1)}, u32[]{:S(2)}, u32[]{:S(2)}) %collective-permute-start.1) | collective-permute-done | bytes 270368 | tf_op jit(solution)/shard_map/ppermute | solution.py:17
  42.0 0.0 copy-start.2
  42.0 0.7 copy-done.2
  42.7 7.1 %shard_map.96 = (f32[512,1024]{1,0:T(8,128)}, f32[512,256]{1,0:T(8,128)}) custom-call(s32[1]{0:T(128)S(6)} %copy.14.info_ref, bf16[512,1024]{1,0:T(8,128)(2,1)} %q_ref.7, bf16[512,1024]{1,0:T(8,128)(2,1)} %do_ref.7, bf16[528,256]{1,0:T(8,128)(2,1)} %copy-done.2, f32[8,512]{1,0:T(8,128)} %lse_ref.7, ...), custom_call_target="tpu_custom_call", output_to_operand_aliasing={{0}: (6, {})} | custom-call | flops 1342177280 | bytes 6553600 | tf_op jit(solution)/shard_map/pallas_call | solution.py:159
  49.9 0.0 collective-permute-done.4
  49.9 1.1 %add.12 = f32[512,256]{1,0:T(8,128)S(1)} add(f32[512,256]{1,0:T(8,128)S(1)} %collective-permute-done.4, f32[512,256]{1,0:T(8,128)} %get-tuple-element.19) | non-fusion elementwise | flops 131072 | bytes 1572864 | tf_op jit(solution)/shard_map/add | solution.py:205
  51.0 2.5 %collective-permute-start.5 = (f32[512,256]{1,0:T(8,128)S(1)}, f32[512,256]{1,0:T(8,128)S(1)}, u32[]{:S(2)}, u32[]{:S(2)}) collective-permute-start(f32[512,256]{1,0:T(8,128)S(1)} %add.12), channel_id=1, source_target_pairs={{0,1},{1,2},{2,3},{3,4},{4,5},{5,6},{6,7},{7,8},{8,9},{9,10},{10,1... | collective-permute-start | bytes 1572872 | tf_op jit(solution)/shard_map/ppermute | solution.py:17
  53.4 0.1 collective-permute-start.2
  53.5 9.0 %collective-permute-done.2.kv_ref = bf16[528,256]{1,0:T(8,128)(2,1)S(1)} collective-permute-done((bf16[528,256]{1,0:T(8,128)(2,1)}, bf16[528,256]{1,0:T(8,128)(2,1)S(1)}, u32[]{:S(2)}, u32[]{:S(2)}) %collective-permute-start.2) | collective-permute-done | bytes 270368 | tf_op jit(solution)/shard_map/ppermute | solution.py:17
  62.6 0.0 copy-start.3
  62.6 0.7 copy-done.3
  63.3 6.7 %shard_map.97 = (bf16[512,1024]{1,0:T(8,128)(2,1)}, f32[512,256]{1,0:T(8,128)}) custom-call(s32[1]{0:T(128)S(6)} %copy.14.info_ref, bf16[512,1024]{1,0:T(8,128)(2,1)} %q_ref.7, bf16[512,1024]{1,0:T(8,128)(2,1)} %do_ref.7, bf16[528,256]{1,0:T(8,128)(2,1)} %copy-done.3, f32[8,512]{1,0:T(8,128)} %lse_ref.7, f32[1,8,512]{2,1,0:T(8,128)} %reshape.12.dl_ref, ...), custom_call_target="tpu_custom_call" | custom-call | flops 1342177280 | bytes 6553600 | tf_op jit(solution)/shard_map/pallas_call | solution.py:159
  70.0 0.0 collective-permute-done.5
  70.0 1.1 %add_convert_fusion = bf16[512,256]{1,0:T(8,128)(2,1)S(1)} fusion(f32[512,256]{1,0:T(8,128)S(1)} %collective-permute-done.5, f32[512,256]{1,0:T(8,128)} %get-tuple-element.20), kind=kLoop, calls=%fused_computation.3 | loop fusion | flops 262144 | bytes 1310720 | tf_op jit(solution)/shard_map/convert_element_type | solution.py:206
  71.1 23.0 %collective-permute-start.6 = (bf16[512,256]{1,0:T(8,128)(2,1)S(1)}, bf16[512,256]{1,0:T(8,128)(2,1)S(1)}, u32[]{:S(2)}, u32[]{:S(2)}) collective-permute-start(bf16[512,256]{1,0:T(8,128)(2,1)S(1)} %add_convert_fusion), channel_id=1, source_target_pairs={{0,253},{1,254},{2,255},{3,0},{4,1},{5,2},{6,3},{7,4},{8,5},{9,6},... | collective-permute-start | bytes 786440 | tf_op jit(solution)/shard_map/ppermute | solution.py:17
  94.2 3.3 %collective-permute-done.6 = bf16[512,256]{1,0:T(8,128)(2,1)S(1)} collective-permute-done((bf16[512,256]{1,0:T(8,128)(2,1)S(1)}, bf16[512,256]{1,0:T(8,128)(2,1)S(1)}, u32[]{:S(2)}, u32[]{:S(2)}) %collective-permute-start.6) | collective-permute-done | bytes 262176 | tf_op jit(solution)/shard_map/ppermute | solution.py:17
  97.5 0.7 fusion.3
Async XLA Ops:
  3.0 9.1 %copy-start = (bf16[528,256]{1,0:T(8,128)(2,1)S(1)}, bf16[528,256]{1,0:T(8,128)(2,1)}, u32[]{:S(2)}) copy-start(bf16[528,256]{1,0:T(8,128)(2,1)} %fusion.2.kv_ref) | copy-start | bytes 811012
  10.3 18.9 %collective-permute-start.3 = (f32[512,256]{1,0:T(8,128)}, f32[512,256]{1,0:T(8,128)S(1)}, u32[]{:S(2)}, u32[]{:S(2)}) collective-permute-start(f32[512,256]{1,0:T(8,128)} %get-tuple-element.17), channel_id=1, source_target_pairs={{0,1},{1,2},{2,3},{3,4},{4,5},{5,6},{6,7},{7,8},{8,9},{9,10},{10,1... | collective-permute-start | bytes 1572872 | tf_op jit(solution)/shard_map/ppermute | solution.py:17
  12.1 9.2 %collective-permute-start = (bf16[528,256]{1,0:T(8,128)(2,1)S(1)}, bf16[528,256]{1,0:T(8,128)(2,1)S(1)}, u32[]{:S(2)}, u32[]{:S(2)}) collective-permute-start(bf16[528,256]{1,0:T(8,128)(2,1)S(1)} %copy-done), channel_id=1, source_target_pairs={{0,1},{1,2},{2,3},{3,4},{4,5},{5,6},{6,7},{7,8},{8,9},{9,10},{10,1... | collective-permute-start | bytes 811016 | tf_op jit(solution)/shard_map/ppermute | solution.py:17
  21.3 0.7 copy-start.1
  30.3 19.6 %collective-permute-start.4 = (f32[512,256]{1,0:T(8,128)S(1)}, f32[512,256]{1,0:T(8,128)S(1)}, u32[]{:S(2)}, u32[]{:S(2)}) collective-permute-start(f32[512,256]{1,0:T(8,128)S(1)} %add.11), channel_id=1, source_target_pairs={{0,1},{1,2},{2,3},{3,4},{4,5},{5,6},{6,7},{7,8},{8,9},{9,10},{10,1... | collective-permute-start | bytes 1572872 | tf_op jit(solution)/shard_map/ppermute | solution.py:17
  32.9 9.1 %collective-permute-start.1 = (bf16[528,256]{1,0:T(8,128)(2,1)}, bf16[528,256]{1,0:T(8,128)(2,1)S(1)}, u32[]{:S(2)}, u32[]{:S(2)}) collective-permute-start(bf16[528,256]{1,0:T(8,128)(2,1)} %copy-done.1), channel_id=1, source_target_pairs={{0,1},{1,2},{2,3},{3,4},{4,5},{5,6},{6,7},{7,8},{8,9},{9,10},{10,1... | collective-permute-start | bytes 811016 | tf_op jit(solution)/shard_map/ppermute | solution.py:17
  42.0 0.7 copy-start.2
  51.0 19.1 %collective-permute-start.5 = (f32[512,256]{1,0:T(8,128)S(1)}, f32[512,256]{1,0:T(8,128)S(1)}, u32[]{:S(2)}, u32[]{:S(2)}) collective-permute-start(f32[512,256]{1,0:T(8,128)S(1)} %add.12), channel_id=1, source_target_pairs={{0,1},{1,2},{2,3},{3,4},{4,5},{5,6},{6,7},{7,8},{8,9},{9,10},{10,1... | collective-permute-start | bytes 1572872 | tf_op jit(solution)/shard_map/ppermute | solution.py:17
  53.4 9.1 %collective-permute-start.2 = (bf16[528,256]{1,0:T(8,128)(2,1)}, bf16[528,256]{1,0:T(8,128)(2,1)S(1)}, u32[]{:S(2)}, u32[]{:S(2)}) collective-permute-start(bf16[528,256]{1,0:T(8,128)(2,1)} %copy-done.2), channel_id=1, source_target_pairs={{0,1},{1,2},{2,3},{3,4},{4,5},{5,6},{6,7},{7,8},{8,9},{9,10},{10,1... | collective-permute-start | bytes 811016 | tf_op jit(solution)/shard_map/ppermute | solution.py:17
  62.6 0.7 copy-start.3
  71.1 26.3 %collective-permute-start.6 = (bf16[512,256]{1,0:T(8,128)(2,1)S(1)}, bf16[512,256]{1,0:T(8,128)(2,1)S(1)}, u32[]{:S(2)}, u32[]{:S(2)}) collective-permute-start(bf16[512,256]{1,0:T(8,128)(2,1)S(1)} %add_convert_fusion), channel_id=1, source_target_pairs={{0,253},{1,254},{2,255},{3,0},{4,1},{5,2},{6,3},{7,4},{8,5},{9,6},... | collective-permute-start | bytes 786440 | tf_op jit(solution)/shard_map/ppermute | solution.py:17
